TPU v7x, 32 devices: a whole 2x2x4 slice. The times are simulated.
32 devices in a mesh: ctx: 16 (over z, y, core), head: 2 (over x).
Axes of the slice: x: 2, y: 2, z: 4, core: 2. Of those that a mesh axis runs over, the one named last changes fastest.
Arguments:
- queries: bfloat16 [4096, 2048], P('ctx', 'head'), may hold values from -160 to 160
- key_rows: bfloat16 [4096, 128], P(('ctx', 'head')), may hold values from -9 to 9
- value_rows: bfloat16 [4096, 128], P(('ctx', 'head')), may hold values from -6 to 6
- span_order: int32 [32], replicated, may hold values from 0 to 31, as said below
- doc_start: int32 [4096], P('ctx'), may hold values from 0 to 3584, as said below
Outputs:
- attended: bfloat16 [4096, 2048], P('ctx', 'head')
Inputs may be any that keep to these rules, and one draw needn't show every extreme that they name: `span_order`: each of 0 to 31 once; entries 2 d and 2 d + 1 are a span c and its mirror 32 - 1 - c. `doc_start`: documents are runs of positions, 6 of them; the first starts at 0 and the last at 3584; row r holds the start of the document of position pos[r].
All inputs are finite; a program needn't handle non-finite values.
Results may differ from a plain program's by a relative error of at most 0.0045.
Values may be sent and summed in bfloat16 or wider, within the bound.
No kernel may reach another device: no remote copies, remote signals or barrier semaphores. Data moves between devices by JAX's collectives and lax.ppermute only.
A program may use at most 192 MiB of HBM per device.

v0:
```python
import functools

import jax
import jax.numpy as jnp
from jax import lax
from jax.experimental import pallas as pl
from jax.experimental.pallas import tpu as pltpu
from jax.sharding import PartitionSpec as P


HEAD_DIM = 128


NEG = -1e30

ORDER_CORE0 = (4, 3, 2, 0)
ORDER_CORE1 = (0, 2, 4, 3)
CORE_BIT = 1


def doubling_gather(block, flat_index, n_dev):
    core = (flat_index >> CORE_BIT) & 1
    held = block
    pieces = []
    for step in range(len(ORDER_CORE0)):
        pairs = []
        for k in range(n_dev):
            bit = ORDER_CORE0[step] if ((k >> CORE_BIT) & 1) == 0 else ORDER_CORE1[step]
            pairs.append((k, k ^ (1 << bit)))
        other = lax.ppermute(held, ("ctx", "head"), pairs)
        if step == len(ORDER_CORE0) - 1:
            pieces.append(held)
            pieces.append(other)
        held = jnp.concatenate([held, other], axis=0)
    other = lax.ppermute(held, ("ctx", "head"), [(k, k ^ (1 << CORE_BIT)) for k in range(n_dev)])
    pieces.append(other)

    def source_mask(order, j):
        mask = 0
        for t, bit in enumerate(order):
            mask = mask | (((j >> t) & 1) << bit)
        return mask

    half = 1 << len(ORDER_CORE0)
    j = jnp.arange(2 * half, dtype=jnp.int32)
    jl = j % half
    own_order_mask = jnp.where(core == 0, source_mask(ORDER_CORE0, jl), source_mask(ORDER_CORE1, jl))
    partner_order_mask = jnp.where(
        core == 0, source_mask(ORDER_CORE1, jl), source_mask(ORDER_CORE0, jl)
    )
    partner = flat_index ^ (1 << CORE_BIT)
    source = jnp.where(j < half, flat_index ^ own_order_mask, partner ^ partner_order_mask)
    return pieces, source


def attend_kernel(info_ref, slot_ref, qt_ref, kv_ref, doc_ref, *rest,
                  heads, span_len, scale, base, first, last):
    rest = list(rest)
    if not first:
        im_ref, il_ref, iacc_ref = rest[:3]
        rest = rest[3:]
    if last:
        o_ref = rest[0]
        rest = rest[1:]
    else:
        om_ref, ol_ref, oacc_ref = rest[:3]
        rest = rest[3:]
    m_ref, l_ref, acc_ref = rest
    j = pl.program_id(0)
    own = info_ref[0, j]
    low = info_ref[1, j]
    full_low = jnp.minimum(info_ref[2, j], own)
    count = kv_ref.shape[0]
    rows = heads * span_len

    if first:
        m_ref[...] = jnp.full(m_ref.shape, NEG, jnp.float32)
        l_ref[...] = jnp.zeros(l_ref.shape, jnp.float32)
        acc_ref[...] = jnp.zeros(acc_ref.shape, jnp.float32)
    else:
        m_ref[...] = im_ref[...]
        l_ref[...] = il_ref[...]
        acc_ref[...] = iacc_ref[...]

    doc_row = doc_ref[...]
    doc = jnp.concatenate([doc_row] * heads, axis=1)
    cols = lax.broadcasted_iota(jnp.int32, (1, rows), 1)
    qpos = own * span_len + lax.rem(cols, span_len)

    def block(p, masked):
        b = slot_ref[p] - base

        @pl.when((b >= 0) & (b < count))
        def _():
            kv = kv_ref[b]
            keys = kv[:, :HEAD_DIM]
            vals_t = kv[:, HEAD_DIM:]
            scores = jnp.dot(keys, qt_ref[...], preferred_element_type=jnp.float32)
            if masked:
                kpos = p * span_len + lax.broadcasted_iota(jnp.int32, (span_len, 1), 0)
                visible = (kpos >= doc) & (kpos <= qpos)
                scores = jnp.where(visible, scores, NEG)
            old_max = m_ref[...]
            new_max = jnp.maximum(old_max, jnp.max(scores, axis=0, keepdims=True))
            rescale = jnp.exp((old_max - new_max) * scale)
            weights = jnp.exp((scores - new_max) * scale)
            if masked:
                weights = jnp.where(visible, weights, 0.0)
            sums = jnp.sum(weights, axis=0, keepdims=True)
            mixed = jnp.dot(vals_t, weights.astype(jnp.bfloat16), preferred_element_type=jnp.float32)
            l_ref[...] = rescale * l_ref[...] + sums
            acc_ref[...] = rescale * acc_ref[...] + mixed
            m_ref[...] = new_max

    block(own, True)

    def masked_step(p, carry):
        block(p, True)
        return carry

    def full_step(p, carry):
        block(p, False)
        return carry

    lax.fori_loop(low, full_low, masked_step, 0)
    lax.fori_loop(jnp.maximum(full_low, low), own, full_step, 0)

    if last:
        out_t = acc_ref[...] / l_ref[...]
        for h in range(heads):
            o_ref[:, h * HEAD_DIM:(h + 1) * HEAD_DIM] = out_t[
                :, h * span_len:(h + 1) * span_len
            ].T.astype(o_ref.dtype)
    else:
        om_ref[...] = m_ref[...]
        ol_ref[...] = l_ref[...]
        oacc_ref[...] = acc_ref[...]


def span_blocks(keys, vals, span_len):
    n = keys.shape[0] // span_len
    vals_t = jnp.swapaxes(vals.reshape(n, span_len, HEAD_DIM), 1, 2)
    return jnp.concatenate([keys.reshape(n, span_len, HEAD_DIM), vals_t], axis=2)


def attend_all(queries, key_rows, value_rows, span_order, doc_start):
    tok_rows = queries.shape[0]
    heads = queries.shape[1] // HEAD_DIM
    kv_count = key_rows.shape[1] // HEAD_DIM
    n_ctx = lax.axis_size("ctx")
    n_head = lax.axis_size("head")
    n_dev = n_ctx * n_head
    ctx_index = lax.axis_index("ctx")
    n_spans = span_order.shape[0]
    length = key_rows.shape[0] * n_dev
    span_len = length // n_spans
    n_local = tok_rows // span_len
    group_index = lax.axis_index("head") * kv_count // n_head
    slot_ids = jnp.arange(n_spans, dtype=jnp.int32)

    if kv_count == 1 and n_dev == 32 and key_rows.shape[0] == span_len:
        flat_index = ctx_index * n_head + lax.axis_index("head")
        local = span_blocks(key_rows, value_rows, span_len)
        pieces, source = doubling_gather(local, flat_index, n_dev)
    else:
        both = jnp.concatenate([key_rows, value_rows], axis=1)
        block_rows = lax.all_gather(both, "head", axis=0, tiled=True)
        own_keys = lax.dynamic_slice_in_dim(block_rows, group_index * HEAD_DIM, HEAD_DIM, 1)
        own_vals = lax.dynamic_slice_in_dim(
            block_rows, (kv_count + group_index) * HEAD_DIM, HEAD_DIM, 1
        )
        local = span_blocks(own_keys, own_vals, span_len)
        whole = lax.all_gather(local, "ctx", axis=0, tiled=True)
        pieces = [whole]
        source = slot_ids

    inverse = jnp.sum(
        jnp.where(span_order[None, :] == slot_ids[:, None], slot_ids[None, :], 0), axis=1
    ).astype(jnp.int32)
    where_held = jnp.sum(
        jnp.where(inverse[:, None] == source[None, :], slot_ids[None, :], 0), axis=1
    ).astype(jnp.int32)

    local_slots = ctx_index * n_local + jnp.arange(n_local, dtype=jnp.int32)
    own_span = jnp.sum(
        jnp.where(local_slots[:, None] == slot_ids[None, :], span_order[None, :], 0), axis=1
    ).astype(jnp.int32)
    doc_spans = doc_start.reshape(n_local, span_len)
    low = jnp.min(doc_spans, axis=1) // span_len
    full_low = (jnp.max(doc_spans, axis=1) + span_len - 1) // span_len
    info = jnp.stack([own_span, low, full_low]).astype(jnp.int32)

    rows = heads * span_len
    doc_rows = doc_start.reshape(n_local, 1, span_len)
    q_t = jnp.transpose(
        queries.reshape(n_local, span_len, heads, HEAD_DIM), (0, 3, 2, 1)
    ).reshape(n_local, HEAD_DIM, rows)

    blocks_est = n_local * (n_spans // 2 + 1)
    state_shapes = [
        jax.ShapeDtypeStruct((n_local, 1, rows), jnp.float32),
        jax.ShapeDtypeStruct((n_local, 1, rows), jnp.float32),
        jax.ShapeDtypeStruct((n_local, HEAD_DIM, rows), jnp.float32),
    ]
    state_specs = [
        pl.BlockSpec((None, 1, rows), lambda j, info, slot: (j, 0, 0)),
        pl.BlockSpec((None, 1, rows), lambda j, info, slot: (j, 0, 0)),
        pl.BlockSpec((None, HEAD_DIM, rows), lambda j, info, slot: (j, 0, 0)),
    ]
    out_shape = jax.ShapeDtypeStruct(queries.shape, queries.dtype)
    out_spec = pl.BlockSpec((span_len, heads * HEAD_DIM), lambda j, info, slot: (j, 0))
    state = None
    base = 0
    for index, piece in enumerate(pieces):
        first = index == 0
        last = index == len(pieces) - 1
        share = piece.shape[0] / n_spans
        kernel = functools.partial(
            attend_kernel, heads=heads, span_len=span_len, scale=HEAD_DIM ** (-0.5),
            base=base, first=first, last=last,
        )
        cost = pl.CostEstimate(
            flops=int(4 * rows * span_len * HEAD_DIM * blocks_est * share),
            transcendentals=int(rows * span_len * blocks_est * share),
            bytes_accessed=2 * queries.size * 2 + piece.size * 2 + 16 * n_local * HEAD_DIM * rows,
        )
        in_specs = [
            pl.BlockSpec((None, HEAD_DIM, rows), lambda j, info, slot: (j, 0, 0)),
            pl.BlockSpec(piece.shape, lambda j, info, slot: (0, 0, 0)),
            pl.BlockSpec((None, 1, span_len), lambda j, info, slot: (j, 0, 0)),
        ]
        operands = [info, where_held, q_t, piece, doc_rows]
        if not first:
            in_specs = in_specs + state_specs
            operands = operands + list(state)
        if last:
            out_shapes, out_specs = out_shape, out_spec
        else:
            out_shapes, out_specs = state_shapes, state_specs
        grid_spec = pltpu.PrefetchScalarGridSpec(
            num_scalar_prefetch=2,
            grid=(n_local,),
            in_specs=in_specs,
            out_specs=out_specs,
            scratch_shapes=[
                pltpu.VMEM((1, rows), jnp.float32),
                pltpu.VMEM((1, rows), jnp.float32),
                pltpu.VMEM((HEAD_DIM, rows), jnp.float32),
            ],
        )
        result = pl.pallas_call(
            kernel,
            grid_spec=grid_spec,
            out_shape=out_shapes,
            compiler_params=pltpu.CompilerParams(dimension_semantics=("arbitrary",)),
            cost_estimate=cost,
        )(*operands)
        base += piece.shape[0]
        if last:
            return result
        state = result


def solution(mesh):
    in_specs = (P("ctx", "head"), P(("ctx", "head"), None), P(("ctx", "head"), None), P(), P("ctx"))
    out_specs = P("ctx", "head")
    return jax.shard_map(
        attend_all, mesh=mesh, in_specs=in_specs, out_specs=out_specs, check_vma=False
    )
```

profile of v0, /device:TPU:16, one launch (start us, length us, event | category | flops | bytes accessed | tf_op | source)
XLA Modules:
  0.0 57.8 jit_solution(4830890184148400994)
XLA Ops:
  0.0 0.0 copy-start.3
  0.0 0.9 %copy.9 = bf16[128,128]{0,1:T(8,128)(2,1)S(1)} copy(bf16[128,128]{1,0:T(8,128)(2,1)} %param.7) | data formatting | bytes 65536 | tf_op args[2]
  0.9 0.0 copy-done.3
  0.9 0.1 collective-permute-start
  1.0 5.2 %collective-permute-done = bf16[1,128,256]{2,1,0:T(8,128)(2,1)S(1)} collective-permute-done((bf16[1,128,256]{2,1,0:T(8,128)(2,1)S(1)}, bf16[1,128,256]{2,1,0:T(8,128)(2,1)S(1)}, u32[]{:S(2)}, u32[]{:S(2)}) %collective-permute-start) | collective-permute-done | bytes 65568 | tf_op jit(solution)/shard_map/ppermute | solution.py:30
  6.2 2.2 %collective-permute-start.1 = (bf16[2,128,256]{2,1,0:T(8,128)(2,1)S(1)}, bf16[2,128,256]{2,1,0:T(8,128)(2,1)S(1)}, u32[]{:S(2)}, u32[]{:S(2)}) collective-permute-start(bf16[2,128,256]{2,1,0:T(8,128)(2,1)S(1)} %pad_maximum_fusion.2), channel_id=1, source_target_pairs={{0,8},{1,9},{2,6},{3,7},{4,12},{5,13},{6,2},{7,3},{8,0},{9,1},{10,... | collective-permute-start | bytes 393224 | tf_op jit(solution)/shard_map/ppermute | solution.py:30
  8.4 3.9 %collective-permute-done.1 = bf16[2,128,256]{2,1,0:T(8,128)(2,1)S(1)} collective-permute-done((bf16[2,128,256]{2,1,0:T(8,128)(2,1)S(1)}, bf16[2,128,256]{2,1,0:T(8,128)(2,1)S(1)}, u32[]{:S(2)}, u32[]{:S(2)}) %collective-permute-start.1) | collective-permute-done | bytes 131104 | tf_op jit(solution)/shard_map/ppermute | solution.py:30
  12.3 1.6 %collective-permute-start.2 = (bf16[4,128,256]{2,1,0:T(8,128)(2,1)S(1)}, bf16[4,128,256]{2,1,0:T(8,128)(2,1)S(1)}, u32[]{:S(2)}, u32[]{:S(2)}) collective-permute-start(bf16[4,128,256]{2,1,0:T(8,128)(2,1)S(1)} %pad_maximum_fusion.1), channel_id=1, source_target_pairs={{0,4},{1,5},{2,18},{3,19},{4,0},{5,1},{6,22},{7,23},{8,12},{9,13},... | collective-permute-start | bytes 786440 | tf_op jit(solution)/shard_map/ppermute | solution.py:30
  13.9 4.9 %collective-permute-done.2 = bf16[4,128,256]{2,1,0:T(8,128)(2,1)S(1)} collective-permute-done((bf16[4,128,256]{2,1,0:T(8,128)(2,1)S(1)}, bf16[4,128,256]{2,1,0:T(8,128)(2,1)S(1)}, u32[]{:S(2)}, u32[]{:S(2)}) %collective-permute-start.2) | collective-permute-done | bytes 262176 | tf_op jit(solution)/shard_map/ppermute | solution.py:30
  18.8 0.0 copy-start.2
  18.8 1.6 %collective-permute-start.3 = (bf16[8,128,256]{2,1,0:T(8,128)(2,1)S(1)}, bf16[8,128,256]{2,1,0:T(8,128)(2,1)S(1)}, u32[]{:S(2)}, u32[]{:S(2)}) collective-permute-start(bf16[8,128,256]{2,1,0:T(8,128)(2,1)S(1)} %pad_maximum_fusion.kv_ref), channel_id=1, source_target_pairs={{0,1},{1,0},{2,10},{3,11},{4,5},{5,4},{6,14},{7,15},{8,9},{9,8},{1... | collective-permute-start | bytes 1572872 | tf_op jit(solution)/shard_map/ppermute | solution.py:30
  20.4 0.0 copy-start.1
  20.4 7.6 %collective-permute-done.3.kv_ref = bf16[8,128,256]{2,1,0:T(8,128)(2,1)S(1)} collective-permute-done((bf16[8,128,256]{2,1,0:T(8,128)(2,1)S(1)}, bf16[8,128,256]{2,1,0:T(8,128)(2,1)S(1)}, u32[]{:S(2)}, u32[]{:S(2)}) %collective-permute-start.3) | collective-permute-done | bytes 524320 | tf_op jit(solution)/shard_map/ppermute | solution.py:30
  28.0 0.0 copy-start
  28.1 0.0 copy-done.2
  28.1 0.7 %copy-done = bf16[8,128,256]{2,1,0:T(8,128)(2,1)} copy-done((bf16[8,128,256]{2,1,0:T(8,128)(2,1)}, bf16[8,128,256]{2,1,0:T(8,128)(2,1)S(1)}, u32[]{:S(2)}) %copy-start) | copy-done | bytes 524312
  28.8 0.0 collective-permute-start.4
  28.8 0.0 copy-done.1
  28.8 0.1 copy.10
  28.9 0.5 copy.8
  29.4 1.0 %reshape.167.qt_ref = bf16[2,128,1024]{2,1,0:T(8,128)(2,1)} reshape(bf16[2,128,8,128]{3,2,1,0:T(8,128)(2,1)S(1)} %bitcast.31) | data formatting | bytes 1048576 | tf_op jit(solution)/shard_map/reshape | solution.py:197
  30.4 0.7 %copy-done.4 = s32[256]{0:T(256)S(1)} copy-done((s32[256]{0:T(256)S(1)}, s32[256]{0:T(256)}, u32[]{:S(2)}) %copy-start.4) | copy-done | bytes 1048
  31.1 0.1 bitcast_reduce_fusion.1
  31.2 0.5 copy-done.5
  31.7 0.2 fusion
  31.9 0.6 %pad_add_fusion.info_ref = s32[3,2]{1,0:T(4,128)} fusion(s32[1,2]{1,0:T(1,128)S(1)} %get-tuple-element.21, s32[1,2]{1,0:T(1,128)S(1)} %get-tuple-element.22, s32[1,2]{1,0:T(1,128)S(1)} %bitcast.45), kind=kLoop, calls=%fused_computation.12 | loop fusion | flops 12 | bytes 48 | tf_op jit(solution)/shard_map/stack | solution.py:191
  32.5 0.1 select_reduce_fusion.1
  32.6 0.7 %select_reduce_fusion.slot_ref = s32[32]{0:T(128)} fusion(s32[32]{0:T(128)S(1)} %compare_select_fusion, s32[32]{0:T(128)S(1)} %select_reduce_fusion.1), kind=kLoop, calls=%fused_computation.4 | loop fusion | flops 3040 | bytes 384 | tf_op jit(solution)/shard_map/reduce_sum | solution.py:180
  33.3 6.7 %shard_map.55 = (f32[2,1,1024]{2,1,0:T(1,128)}, f32[2,1,1024]{2,1,0:T(1,128)}, f32[2,128,1024]{2,1,0:T(8,128)}) custom-call(s32[3,2]{1,0:T(4,128)} %pad_add_fusion.info_ref, s32[32]{0:T(128)} %select_reduce_fusion.slot_ref, bf16[2,128,1024]{2,1,0:T(8,128)(2,1)} %reshape.167.qt_ref, bf16[8,128,256]{2,1,0:T(8,128)(2,1)} %copy-done.2, s32[2,1,128]{2,1,0:T(1,128)} %bitcast.42), custom_call_target="tpu_custom_call" | custom-call | flops 570425344 | bytes 5767168 | tf_op jit(solution)/shard_map/pallas_call | solution.py:251
  40.1 6.2 %shard_map.56 = (f32[2,1,1024]{2,1,0:T(1,128)}, f32[2,1,1024]{2,1,0:T(1,128)}, f32[2,128,1024]{2,1,0:T(8,128)}) custom-call(s32[3,2]{1,0:T(4,128)} %pad_add_fusion.info_ref, s32[32]{0:T(128)} %select_reduce_fusion.slot_ref, bf16[2,128,1024]{2,1,0:T(8,128)(2,1)} %reshape.167.qt_ref, bf16[8,128,256]{2,1,0:T(8,128)(2,1)} %copy-done, s32[2,1,128]{2,1,0:T(1,128)} %bitcast.43, ...), custom_call_target="tpu_custom_call" | custom-call | flops 570425344 | bytes 5767168 | tf_op jit(solution)/shard_map/pallas_call | solution.py:251
  46.3 0.0 collective-permute-done.4.kv_ref
  46.3 11.5 %shard_map.57 = bf16[256,1024]{1,0:T(8,128)(2,1)} custom-call(s32[3,2]{1,0:T(4,128)} %pad_add_fusion.info_ref, s32[32]{0:T(128)} %select_reduce_fusion.slot_ref, bf16[2,128,1024]{2,1,0:T(8,128)(2,1)} %reshape.167.qt_ref, bf16[16,128,256]{2,1,0:T(8,128)(2,1)} %collective-permute-done.4.kv_ref, s32[2,1,128]{2,1,0:T(1,128)} %bitcast.44, ...), custom_call_target="tpu_custom_call" | custom-call | flops 1140850688 | bytes 6291456 | tf_op jit(solution)/shard_map/pallas_call | solution.py:251
  (13 shorter events, 0.2 us)
Async XLA Ops:
  0.0 0.9 %copy-start.3 = (bf16[128,128]{1,0:T(8,128)(2,1)S(1)}, bf16[128,128]{1,0:T(8,128)(2,1)}, u32[]{:S(2)}) copy-start(bf16[128,128]{1,0:T(8,128)(2,1)} %param.6) | copy-start | bytes 98308
  0.9 5.3 %collective-permute-start = (bf16[1,128,256]{2,1,0:T(8,128)(2,1)S(1)}, bf16[1,128,256]{2,1,0:T(8,128)(2,1)S(1)}, u32[]{:S(2)}, u32[]{:S(2)}) collective-permute-start(bf16[1,128,256]{2,1,0:T(8,128)(2,1)S(1)} %get-tuple-element.19), channel_id=1, source_target_pairs={{0,16},{1,17},{2,3},{3,2},{4,20},{5,21},{6,7},{7,6},{8,24},{9,25},... | collective-permute-start | bytes 196616 | tf_op jit(solution)/shard_map/ppermute | solution.py:30
  6.2 6.1 %collective-permute-start.1 = (bf16[2,128,256]{2,1,0:T(8,128)(2,1)S(1)}, bf16[2,128,256]{2,1,0:T(8,128)(2,1)S(1)}, u32[]{:S(2)}, u32[]{:S(2)}) collective-permute-start(bf16[2,128,256]{2,1,0:T(8,128)(2,1)S(1)} %pad_maximum_fusion.2), channel_id=1, source_target_pairs={{0,8},{1,9},{2,6},{3,7},{4,12},{5,13},{6,2},{7,3},{8,0},{9,1},{10,... | collective-permute-start | bytes 393224 | tf_op jit(solution)/shard_map/ppermute | solution.py:30
  12.3 6.4 %collective-permute-start.2 = (bf16[4,128,256]{2,1,0:T(8,128)(2,1)S(1)}, bf16[4,128,256]{2,1,0:T(8,128)(2,1)S(1)}, u32[]{:S(2)}, u32[]{:S(2)}) collective-permute-start(bf16[4,128,256]{2,1,0:T(8,128)(2,1)S(1)} %pad_maximum_fusion.1), channel_id=1, source_target_pairs={{0,4},{1,5},{2,18},{3,19},{4,0},{5,1},{6,22},{7,23},{8,12},{9,13},... | collective-permute-start | bytes 786440 | tf_op jit(solution)/shard_map/ppermute | solution.py:30
  18.8 9.3 %copy-start.2 = (bf16[8,128,256]{2,1,0:T(8,128)(2,1)}, bf16[8,128,256]{2,1,0:T(8,128)(2,1)S(1)}, u32[]{:S(2)}) copy-start(bf16[8,128,256]{2,1,0:T(8,128)(2,1)S(1)} %pad_maximum_fusion.kv_ref) | copy-start | bytes 1572868
  18.8 9.2 %collective-permute-start.3 = (bf16[8,128,256]{2,1,0:T(8,128)(2,1)S(1)}, bf16[8,128,256]{2,1,0:T(8,128)(2,1)S(1)}, u32[]{:S(2)}, u32[]{:S(2)}) collective-permute-start(bf16[8,128,256]{2,1,0:T(8,128)(2,1)S(1)} %pad_maximum_fusion.kv_ref), channel_id=1, source_target_pairs={{0,1},{1,0},{2,10},{3,11},{4,5},{5,4},{6,14},{7,15},{8,9},{9,8},{1... | collective-permute-start | bytes 1572872 | tf_op jit(solution)/shard_map/ppermute | solution.py:30
  20.4 8.4 %copy-start.1 = (bf16[256,1024]{1,0:T(8,128)(2,1)S(1)}, bf16[256,1024]{1,0:T(8,128)(2,1)}, u32[]{:S(2)}) copy-start(bf16[256,1024]{1,0:T(8,128)(2,1)} %param.5) | copy-start | bytes 1572868
  28.0 0.8 %copy-start = (bf16[8,128,256]{2,1,0:T(8,128)(2,1)}, bf16[8,128,256]{2,1,0:T(8,128)(2,1)S(1)}, u32[]{:S(2)}) copy-start(bf16[8,128,256]{2,1,0:T(8,128)(2,1)S(1)} %collective-permute-done.3.kv_ref) | copy-start | bytes 1572868
  28.8 17.5 %collective-permute-start.4 = (bf16[16,128,256]{2,1,0:T(8,128)(2,1)S(1)}, bf16[16,128,256]{2,1,0:T(8,128)(2,1)}, u32[]{:S(2)}, u32[]{:S(2)}) collective-permute-start(bf16[16,128,256]{2,1,0:T(8,128)(2,1)S(1)} %constant_dynamic-update-slice_fusion), channel_id=1, source_target_pairs={{0,2},{1,3},{2,0},{3,1},{4,6},{5,7},{6,4},{7,5},{8,10},{9,11},{10,... | collective-permute-start | bytes 3145736 | tf_op jit(solution)/shard_map/ppermute | solution.py:35
  30.4 0.7 %copy-start.4 = (s32[256]{0:T(256)S(1)}, s32[256]{0:T(256)}, u32[]{:S(2)}) copy-start(s32[256]{0:T(256)} %param.9) | copy-start | bytes 3076
  31.1 0.7 %copy-start.5 = (s32[32]{0:T(128)S(1)}, s32[32]{0:T(128)}, u32[]{:S(2)}) copy-start(s32[32]{0:T(128)} %param.8) | copy-start | bytes 388
where the time goes:
time: 58.2 us; the launch traced here: 57.8 us
  Pallas kernels  24.5 us (42%)
  waiting for transfers between devices  21.6 us (37%)
  starting transfers between devices  5.38 us (9%)
  local copies, waits for them, and re-layouts  4.43 us (8%)
  other arithmetic  1.84 us (3%)
    pallas_call x3, Pallas kernels, attend_all(): pl.pallas_call(kernel, grid_spec=grid_spec, out_shape=out_shapes, compile...  24.5 us
    ppermute x4, waiting for transfers between devices, doubling_gather(): other = lax.ppermute(held, ('ctx', 'head'), pairs)  21.6 us
    ppermute x4, starting transfers between devices, doubling_gather(): other = lax.ppermute(held, ('ctx', 'head'), pairs)  5.38 us
    unnamed x17, local copies, waits for them, and re-layouts  2.93 us
  transfers between devices with their start and end apart: 5, of which 4 were waited for; matrix products, arithmetic and copies ran while one was open for 6% of the time, Pallas kernels for 22%

commit v1 on v0

--- a/solution.py
+++ b/solution.py
@@ -54,87 +54,83 @@
 
 
 def attend_kernel(info_ref, slot_ref, qt_ref, kv_ref, doc_ref, *rest,
-                  heads, span_len, scale, base, first, last):
+                  heads, span_len, scale, base, first, last, n_local):
     rest = list(rest)
     if not first:
-        im_ref, il_ref, iacc_ref = rest[:3]
+        im_all, il_all, iacc_all = rest[:3]
         rest = rest[3:]
-    if last:
-        o_ref = rest[0]
-        rest = rest[1:]
-    else:
-        om_ref, ol_ref, oacc_ref = rest[:3]
-        rest = rest[3:]
-    m_ref, l_ref, acc_ref = rest
-    j = pl.program_id(0)
-    own = info_ref[0, j]
-    low = info_ref[1, j]
-    full_low = jnp.minimum(info_ref[2, j], own)
+    m_all, l_all, acc_all = rest[:3]
+    o_ref = rest[3] if last else None
     count = kv_ref.shape[0]
     rows = heads * span_len
-
-    if first:
-        m_ref[...] = jnp.full(m_ref.shape, NEG, jnp.float32)
-        l_ref[...] = jnp.zeros(l_ref.shape, jnp.float32)
-        acc_ref[...] = jnp.zeros(acc_ref.shape, jnp.float32)
-    else:
-        m_ref[...] = im_ref[...]
-        l_ref[...] = il_ref[...]
-        acc_ref[...] = iacc_ref[...]
-
-    doc_row = doc_ref[...]
-    doc = jnp.concatenate([doc_row] * heads, axis=1)
     cols = lax.broadcasted_iota(jnp.int32, (1, rows), 1)
-    qpos = own * span_len + lax.rem(cols, span_len)
-
-    def block(p, masked):
-        b = slot_ref[p] - base
-
-        @pl.when((b >= 0) & (b < count))
-        def _():
-            kv = kv_ref[b]
-            keys = kv[:, :HEAD_DIM]
-            vals_t = kv[:, HEAD_DIM:]
-            scores = jnp.dot(keys, qt_ref[...], preferred_element_type=jnp.float32)
-            if masked:
-                kpos = p * span_len + lax.broadcasted_iota(jnp.int32, (span_len, 1), 0)
-                visible = (kpos >= doc) & (kpos <= qpos)
-                scores = jnp.where(visible, scores, NEG)
-            old_max = m_ref[...]
-            new_max = jnp.maximum(old_max, jnp.max(scores, axis=0, keepdims=True))
-            rescale = jnp.exp((old_max - new_max) * scale)
-            weights = jnp.exp((scores - new_max) * scale)
-            if masked:
-                weights = jnp.where(visible, weights, 0.0)
-            sums = jnp.sum(weights, axis=0, keepdims=True)
-            mixed = jnp.dot(vals_t, weights.astype(jnp.bfloat16), preferred_element_type=jnp.float32)
-            l_ref[...] = rescale * l_ref[...] + sums
-            acc_ref[...] = rescale * acc_ref[...] + mixed
-            m_ref[...] = new_max
-
-    block(own, True)
-
-    def masked_step(p, carry):
-        block(p, True)
-        return carry
-
-    def full_step(p, carry):
-        block(p, False)
-        return carry
-
-    lax.fori_loop(low, full_low, masked_step, 0)
-    lax.fori_loop(jnp.maximum(full_low, low), own, full_step, 0)
-
-    if last:
-        out_t = acc_ref[...] / l_ref[...]
-        for h in range(heads):
-            o_ref[:, h * HEAD_DIM:(h + 1) * HEAD_DIM] = out_t[
-                :, h * span_len:(h + 1) * span_len
-            ].T.astype(o_ref.dtype)
-    else:
-        om_ref[...] = m_ref[...]
-        ol_ref[...] = l_ref[...]
-        oacc_ref[...] = acc_ref[...]
+
+    for j in range(n_local):
+        own = info_ref[0, j]
+        low = info_ref[1, j]
+        full_low = jnp.minimum(info_ref[2, j], own)
+        m_ref = m_all.at[j]
+        l_ref = l_all.at[j]
+        acc_ref = acc_all.at[j]
+        qt_ref_j = qt_ref.at[j]
+
+        if first:
+            m_ref[...] = jnp.full(m_ref.shape, NEG, jnp.float32)
+            l_ref[...] = jnp.zeros(l_ref.shape, jnp.float32)
+            acc_ref[...] = jnp.zeros(acc_ref.shape, jnp.float32)
+        else:
+            m_ref[...] = im_all[j]
+            l_ref[...] = il_all[j]
+            acc_ref[...] = iacc_all[j]
+
+        doc = jnp.concatenate([doc_ref[j]] * heads, axis=1)
+        qpos = own * span_len + lax.rem(cols, span_len)
+
+        def block(p, masked, m_ref=m_ref, l_ref=l_ref, acc_ref=acc_ref, qt_ref_j=qt_ref_j,
+                  doc=doc, qpos=qpos):
+            b = slot_ref[p] - base
+
+            @pl.when((b >= 0) & (b < count))
+            def _():
+                kv = kv_ref[b]
+                keys = kv[:, :HEAD_DIM]
+                vals_t = kv[:, HEAD_DIM:]
+                scores = jnp.dot(keys, qt_ref_j[...], preferred_element_type=jnp.float32)
+                if masked:
+                    kpos = p * span_len + lax.broadcasted_iota(jnp.int32, (span_len, 1), 0)
+                    visible = (kpos >= doc) & (kpos <= qpos)
+                    scores = jnp.where(visible, scores, NEG)
+                old_max = m_ref[...]
+                new_max = jnp.maximum(old_max, jnp.max(scores, axis=0, keepdims=True))
+                rescale = jnp.exp((old_max - new_max) * scale)
+                weights = jnp.exp((scores - new_max) * scale)
+                if masked:
+                    weights = jnp.where(visible, weights, 0.0)
+                sums = jnp.sum(weights, axis=0, keepdims=True)
+                mixed = jnp.dot(vals_t, weights.astype(jnp.bfloat16), preferred_element_type=jnp.float32)
+                l_ref[...] = rescale * l_ref[...] + sums
+                acc_ref[...] = rescale * acc_ref[...] + mixed
+                m_ref[...] = new_max
+
+        block(own, True)
+
+        def masked_step(p, carry, block=block):
+            block(p, True)
+            return carry
+
+        def full_step(p, carry, block=block):
+            block(p, False)
+            return carry
+
+        lax.fori_loop(low, full_low, masked_step, 0)
+        lax.fori_loop(jnp.maximum(full_low, low), own, full_step, 0)
+
+        if last:
+            out_t = acc_ref[...] / l_ref[...]
+            for h in range(heads):
+                o_ref[j * span_len:(j + 1) * span_len, h * HEAD_DIM:(h + 1) * HEAD_DIM] = out_t[
+                    :, h * span_len:(h + 1) * span_len
+                ].T.astype(o_ref.dtype)
 
 
 def span_blocks(keys, vals, span_len):
@@ -202,13 +198,9 @@
         jax.ShapeDtypeStruct((n_local, 1, rows), jnp.float32),
         jax.ShapeDtypeStruct((n_local, HEAD_DIM, rows), jnp.float32),
     ]
-    state_specs = [
-        pl.BlockSpec((None, 1, rows), lambda j, info, slot: (j, 0, 0)),
-        pl.BlockSpec((None, 1, rows), lambda j, info, slot: (j, 0, 0)),
-        pl.BlockSpec((None, HEAD_DIM, rows), lambda j, info, slot: (j, 0, 0)),
-    ]
     out_shape = jax.ShapeDtypeStruct(queries.shape, queries.dtype)
-    out_spec = pl.BlockSpec((span_len, heads * HEAD_DIM), lambda j, info, slot: (j, 0))
+    vmem = pl.BlockSpec(memory_space=pltpu.VMEM)
+    smem = pl.BlockSpec(memory_space=pltpu.SMEM)
     state = None
     base = 0
     for index, piece in enumerate(pieces):
@@ -217,48 +209,30 @@
         share = piece.shape[0] / n_spans
         kernel = functools.partial(
             attend_kernel, heads=heads, span_len=span_len, scale=HEAD_DIM ** (-0.5),
-            base=base, first=first, last=last,
+            base=base, first=first, last=last, n_local=n_local,
         )
         cost = pl.CostEstimate(
             flops=int(4 * rows * span_len * HEAD_DIM * blocks_est * share),
             transcendentals=int(rows * span_len * blocks_est * share),
-            bytes_accessed=2 * queries.size * 2 + piece.size * 2 + 16 * n_local * HEAD_DIM * rows,
+            bytes_accessed=2 * queries.size * 2 + piece.size * 2,
         )
-        in_specs = [
-            pl.BlockSpec((None, HEAD_DIM, rows), lambda j, info, slot: (j, 0, 0)),
-            pl.BlockSpec(piece.shape, lambda j, info, slot: (0, 0, 0)),
-            pl.BlockSpec((None, 1, span_len), lambda j, info, slot: (j, 0, 0)),
-        ]
         operands = [info, where_held, q_t, piece, doc_rows]
+        in_specs = [smem, smem, vmem, vmem, vmem]
         if not first:
-            in_specs = in_specs + state_specs
             operands = operands + list(state)
-        if last:
-            out_shapes, out_specs = out_shape, out_spec
-        else:
-            out_shapes, out_specs = state_shapes, state_specs
-        grid_spec = pltpu.PrefetchScalarGridSpec(
-            num_scalar_prefetch=2,
-            grid=(n_local,),
-            in_specs=in_specs,
-            out_specs=out_specs,
-            scratch_shapes=[
-                pltpu.VMEM((1, rows), jnp.float32),
-                pltpu.VMEM((1, rows), jnp.float32),
-                pltpu.VMEM((HEAD_DIM, rows), jnp.float32),
-            ],
-        )
+            in_specs = in_specs + [vmem] * 3
+        out_shapes = list(state_shapes) + ([out_shape] if last else [])
         result = pl.pallas_call(
             kernel,
-            grid_spec=grid_spec,
+            in_specs=in_specs,
+            out_specs=[vmem] * len(out_shapes),
             out_shape=out_shapes,
-            compiler_params=pltpu.CompilerParams(dimension_semantics=("arbitrary",)),
             cost_estimate=cost,
         )(*operands)
         base += piece.shape[0]
         if last:
-            return result
-        state = result
+            return result[3]
+        state = result[:3]
 
 
 def solution(mesh):

time: 58.2 us -> 57 us (0.979)
  Pallas kernels: 24.5 us -> 23.3 us
    pallas_call x3, Pallas kernels: 24.5 us -> 23.3 us  [attend_all(): pl.pallas_call(kernel, in_specs=in_specs, out_specs=[vmem] * len(out_shap...]
  transfers between devices with their start and end apart: 5 -> 5, of which waited for: 4 -> 4; matrix products, arithmetic and copies ran while one was open for 6% -> 6% of each run, Pallas kernels for 22% -> 21%
where the time goes in v1:
time: 57 us; the launch traced here: 56.7 us
  Pallas kernels  23.3 us (41%)
  waiting for transfers between devices  21.6 us (38%)
  starting transfers between devices  5.38 us (9%)
  local copies, waits for them, and re-layouts  4.44 us (8%)
  other arithmetic  1.9 us (3%)
    pallas_call x3, Pallas kernels, attend_all(): pl.pallas_call(kernel, in_specs=in_specs, out_specs=[vmem] * len(out_shap...  23.3 us
    ppermute x4, waiting for transfers between devices, doubling_gather(): other = lax.ppermute(held, ('ctx', 'head'), pairs)  21.6 us
    ppermute x4, starting transfers between devices, doubling_gather(): other = lax.ppermute(held, ('ctx', 'head'), pairs)  5.38 us
    unnamed x17, local copies, waits for them, and re-layouts  2.93 us
  transfers between devices with their start and end apart: 5, of which 4 were waited for; matrix products, arithmetic and copies ran while one was open for 6% of the time, Pallas kernels for 21%

profile of v1, /device:TPU:16, one launch (start us, length us, event | category | flops | bytes accessed | tf_op | source)
XLA Modules:
  0.0 56.7 jit_solution(7917349290759746831)
XLA Ops:
  0.0 0.0 copy-start.3
  0.0 0.9 %copy.9 = bf16[128,128]{0,1:T(8,128)(2,1)S(1)} copy(bf16[128,128]{1,0:T(8,128)(2,1)} %param.7) | data formatting | bytes 65536 | tf_op args[2]
  0.9 0.0 copy-done.3
  0.9 0.1 collective-permute-start
  1.0 5.2 %collective-permute-done = bf16[1,128,256]{2,1,0:T(8,128)(2,1)S(1)} collective-permute-done((bf16[1,128,256]{2,1,0:T(8,128)(2,1)S(1)}, bf16[1,128,256]{2,1,0:T(8,128)(2,1)S(1)}, u32[]{:S(2)}, u32[]{:S(2)}) %collective-permute-start) | collective-permute-done | bytes 65568 | tf_op jit(solution)/shard_map/ppermute | solution.py:30
  6.2 2.2 %collective-permute-start.1 = (bf16[2,128,256]{2,1,0:T(8,128)(2,1)S(1)}, bf16[2,128,256]{2,1,0:T(8,128)(2,1)S(1)}, u32[]{:S(2)}, u32[]{:S(2)}) collective-permute-start(bf16[2,128,256]{2,1,0:T(8,128)(2,1)S(1)} %pad_maximum_fusion.2), channel_id=1, source_target_pairs={{0,8},{1,9},{2,6},{3,7},{4,12},{5,13},{6,2},{7,3},{8,0},{9,1},{10,... | collective-permute-start | bytes 393224 | tf_op jit(solution)/shard_map/ppermute | solution.py:30
  8.4 3.9 %collective-permute-done.1 = bf16[2,128,256]{2,1,0:T(8,128)(2,1)S(1)} collective-permute-done((bf16[2,128,256]{2,1,0:T(8,128)(2,1)S(1)}, bf16[2,128,256]{2,1,0:T(8,128)(2,1)S(1)}, u32[]{:S(2)}, u32[]{:S(2)}) %collective-permute-start.1) | collective-permute-done | bytes 131104 | tf_op jit(solution)/shard_map/ppermute | solution.py:30
  12.3 1.6 %collective-permute-start.2 = (bf16[4,128,256]{2,1,0:T(8,128)(2,1)S(1)}, bf16[4,128,256]{2,1,0:T(8,128)(2,1)S(1)}, u32[]{:S(2)}, u32[]{:S(2)}) collective-permute-start(bf16[4,128,256]{2,1,0:T(8,128)(2,1)S(1)} %pad_maximum_fusion.1), channel_id=1, source_target_pairs={{0,4},{1,5},{2,18},{3,19},{4,0},{5,1},{6,22},{7,23},{8,12},{9,13},... | collective-permute-start | bytes 786440 | tf_op jit(solution)/shard_map/ppermute | solution.py:30
  13.9 4.9 %collective-permute-done.2 = bf16[4,128,256]{2,1,0:T(8,128)(2,1)S(1)} collective-permute-done((bf16[4,128,256]{2,1,0:T(8,128)(2,1)S(1)}, bf16[4,128,256]{2,1,0:T(8,128)(2,1)S(1)}, u32[]{:S(2)}, u32[]{:S(2)}) %collective-permute-start.2) | collective-permute-done | bytes 262176 | tf_op jit(solution)/shard_map/ppermute | solution.py:30
  18.8 0.0 copy-start.2
  18.8 1.6 %collective-permute-start.3 = (bf16[8,128,256]{2,1,0:T(8,128)(2,1)S(1)}, bf16[8,128,256]{2,1,0:T(8,128)(2,1)S(1)}, u32[]{:S(2)}, u32[]{:S(2)}) collective-permute-start(bf16[8,128,256]{2,1,0:T(8,128)(2,1)S(1)} %pad_maximum_fusion.kv_ref), channel_id=1, source_target_pairs={{0,1},{1,0},{2,10},{3,11},{4,5},{5,4},{6,14},{7,15},{8,9},{9,8},{1... | collective-permute-start | bytes 1572872 | tf_op jit(solution)/shard_map/ppermute | solution.py:30
  20.4 0.0 copy-start.1
  20.4 7.6 %collective-permute-done.3.kv_ref = bf16[8,128,256]{2,1,0:T(8,128)(2,1)S(1)} collective-permute-done((bf16[8,128,256]{2,1,0:T(8,128)(2,1)S(1)}, bf16[8,128,256]{2,1,0:T(8,128)(2,1)S(1)}, u32[]{:S(2)}, u32[]{:S(2)}) %collective-permute-start.3) | collective-permute-done | bytes 524320 | tf_op jit(solution)/shard_map/ppermute | solution.py:30
  28.0 0.0 copy-start
  28.1 0.0 copy-done.2
  28.1 0.7 %copy-done = bf16[8,128,256]{2,1,0:T(8,128)(2,1)} copy-done((bf16[8,128,256]{2,1,0:T(8,128)(2,1)}, bf16[8,128,256]{2,1,0:T(8,128)(2,1)S(1)}, u32[]{:S(2)}) %copy-start) | copy-done | bytes 524312
  28.8 0.0 collective-permute-start.4
  28.8 0.0 copy-done.1
  28.8 0.1 copy.10
  28.9 0.5 copy.8
  29.4 1.0 %reshape.167.qt_ref = bf16[2,128,1024]{2,1,0:T(8,128)(2,1)} reshape(bf16[2,128,8,128]{3,2,1,0:T(8,128)(2,1)S(1)} %bitcast.31) | data formatting | bytes 1048576 | tf_op jit(solution)/shard_map/reshape | solution.py:193
  30.4 0.7 %copy-done.4 = s32[256]{0:T(256)S(1)} copy-done((s32[256]{0:T(256)S(1)}, s32[256]{0:T(256)}, u32[]{:S(2)}) %copy-start.4) | copy-done | bytes 1048
  31.1 0.1 bitcast_reduce_fusion.1
  31.2 0.5 copy-done.5
  31.7 0.2 fusion
  31.9 0.6 %pad_add_fusion.info_ref = s32[3,2]{1,0:T(4,128)} fusion(s32[1,2]{1,0:T(1,128)S(1)} %get-tuple-element.23, s32[1,2]{1,0:T(1,128)S(1)} %get-tuple-element.24, s32[1,2]{1,0:T(1,128)S(1)} %bitcast.45), kind=kLoop, calls=%fused_computation.12 | loop fusion | flops 12 | bytes 48 | tf_op jit(solution)/shard_map/stack | solution.py:187
  32.5 0.1 select_reduce_fusion.1
  32.7 0.8 %select_reduce_fusion.slot_ref = s32[32]{0:T(128)} fusion(s32[32]{0:T(128)S(1)} %compare_select_fusion, s32[32]{0:T(128)S(1)} %select_reduce_fusion.1), kind=kLoop, calls=%fused_computation.4 | loop fusion | flops 3040 | bytes 384 | tf_op jit(solution)/shard_map/reduce_sum | solution.py:176
  33.4 6.2 %shard_map.55 = (f32[2,1,1024]{2,1,0:T(1,128)}, f32[2,1,1024]{2,1,0:T(1,128)}, f32[2,128,1024]{2,1,0:T(8,128)}) custom-call(s32[3,2]{1,0:T(4,128)} %pad_add_fusion.info_ref, s32[32]{0:T(128)} %select_reduce_fusion.slot_ref, bf16[2,128,1024]{2,1,0:T(8,128)(2,1)} %reshape.167.qt_ref, bf16[8,128,256]{2,1,0:T(8,128)(2,1)} %copy-done.2, s32[2,1,128]{2,1,0:T(1,128)} %bitcast.42), custom_call_target="tpu_custom_call" | custom-call | flops 570425344 | bytes 1572864 | tf_op jit(solution)/shard_map/pallas_call | solution.py:225
  39.6 5.9 %shard_map.56 = (f32[2,1,1024]{2,1,0:T(1,128)}, f32[2,1,1024]{2,1,0:T(1,128)}, f32[2,128,1024]{2,1,0:T(8,128)}) custom-call(s32[3,2]{1,0:T(4,128)} %pad_add_fusion.info_ref, s32[32]{0:T(128)} %select_reduce_fusion.slot_ref, bf16[2,128,1024]{2,1,0:T(8,128)(2,1)} %reshape.167.qt_ref, bf16[8,128,256]{2,1,0:T(8,128)(2,1)} %copy-done, s32[2,1,128]{2,1,0:T(1,128)} %bitcast.43, ...), custom_call_target="tpu_custom_call" | custom-call | flops 570425344 | bytes 1572864 | tf_op jit(solution)/shard_map/pallas_call | solution.py:225
  45.5 0.0 collective-permute-done.4.kv_ref
  45.5 11.2 %shard_map.57 = (f32[2,1,1024]{2,1,0:T(1,128)}, f32[2,1,1024]{2,1,0:T(1,128)}, f32[2,128,1024]{2,1,0:T(8,128)}, bf16[256,1024]{1,0:T(8,128)(2,1)}) custom-call(s32[3,2]{1,0:T(4,128)} %pad_add_fusion.info_ref, s32[32]{0:T(128)} %select_reduce_fusion.slot_ref, bf16[2,128,1024]{2,1,0:T(8,128)(2,1)} %reshape.167.qt_ref, ...), custom_call_target="tpu_custom_call" | custom-call | flops 1140850688 | bytes 2097152 | tf_op jit(solution)/shard_map/pallas_call | solution.py:225
  (13 shorter events, 0.2 us)
Async XLA Ops:
  0.0 0.9 %copy-start.3 = (bf16[128,128]{1,0:T(8,128)(2,1)S(1)}, bf16[128,128]{1,0:T(8,128)(2,1)}, u32[]{:S(2)}) copy-start(bf16[128,128]{1,0:T(8,128)(2,1)} %param.6) | copy-start | bytes 98308
  0.9 5.3 %collective-permute-start = (bf16[1,128,256]{2,1,0:T(8,128)(2,1)S(1)}, bf16[1,128,256]{2,1,0:T(8,128)(2,1)S(1)}, u32[]{:S(2)}, u32[]{:S(2)}) collective-permute-start(bf16[1,128,256]{2,1,0:T(8,128)(2,1)S(1)} %get-tuple-element.21), channel_id=1, source_target_pairs={{0,16},{1,17},{2,3},{3,2},{4,20},{5,21},{6,7},{7,6},{8,24},{9,25},... | collective-permute-start | bytes 196616 | tf_op jit(solution)/shard_map/ppermute | solution.py:30
  6.2 6.1 %collective-permute-start.1 = (bf16[2,128,256]{2,1,0:T(8,128)(2,1)S(1)}, bf16[2,128,256]{2,1,0:T(8,128)(2,1)S(1)}, u32[]{:S(2)}, u32[]{:S(2)}) collective-permute-start(bf16[2,128,256]{2,1,0:T(8,128)(2,1)S(1)} %pad_maximum_fusion.2), channel_id=1, source_target_pairs={{0,8},{1,9},{2,6},{3,7},{4,12},{5,13},{6,2},{7,3},{8,0},{9,1},{10,... | collective-permute-start | bytes 393224 | tf_op jit(solution)/shard_map/ppermute | solution.py:30
  12.3 6.4 %collective-permute-start.2 = (bf16[4,128,256]{2,1,0:T(8,128)(2,1)S(1)}, bf16[4,128,256]{2,1,0:T(8,128)(2,1)S(1)}, u32[]{:S(2)}, u32[]{:S(2)}) collective-permute-start(bf16[4,128,256]{2,1,0:T(8,128)(2,1)S(1)} %pad_maximum_fusion.1), channel_id=1, source_target_pairs={{0,4},{1,5},{2,18},{3,19},{4,0},{5,1},{6,22},{7,23},{8,12},{9,13},... | collective-permute-start | bytes 786440 | tf_op jit(solution)/shard_map/ppermute | solution.py:30
  18.8 9.3 %copy-start.2 = (bf16[8,128,256]{2,1,0:T(8,128)(2,1)}, bf16[8,128,256]{2,1,0:T(8,128)(2,1)S(1)}, u32[]{:S(2)}) copy-start(bf16[8,128,256]{2,1,0:T(8,128)(2,1)S(1)} %pad_maximum_fusion.kv_ref) | copy-start | bytes 1572868
  18.8 9.2 %collective-permute-start.3 = (bf16[8,128,256]{2,1,0:T(8,128)(2,1)S(1)}, bf16[8,128,256]{2,1,0:T(8,128)(2,1)S(1)}, u32[]{:S(2)}, u32[]{:S(2)}) collective-permute-start(bf16[8,128,256]{2,1,0:T(8,128)(2,1)S(1)} %pad_maximum_fusion.kv_ref), channel_id=1, source_target_pairs={{0,1},{1,0},{2,10},{3,11},{4,5},{5,4},{6,14},{7,15},{8,9},{9,8},{1... | collective-permute-start | bytes 1572872 | tf_op jit(solution)/shard_map/ppermute | solution.py:30
  20.4 8.4 %copy-start.1 = (bf16[256,1024]{1,0:T(8,128)(2,1)S(1)}, bf16[256,1024]{1,0:T(8,128)(2,1)}, u32[]{:S(2)}) copy-start(bf16[256,1024]{1,0:T(8,128)(2,1)} %param.5) | copy-start | bytes 1572868
  28.0 0.8 %copy-start = (bf16[8,128,256]{2,1,0:T(8,128)(2,1)}, bf16[8,128,256]{2,1,0:T(8,128)(2,1)S(1)}, u32[]{:S(2)}) copy-start(bf16[8,128,256]{2,1,0:T(8,128)(2,1)S(1)} %collective-permute-done.3.kv_ref) | copy-start | bytes 1572868
  28.8 16.7 %collective-permute-start.4 = (bf16[16,128,256]{2,1,0:T(8,128)(2,1)S(1)}, bf16[16,128,256]{2,1,0:T(8,128)(2,1)}, u32[]{:S(2)}, u32[]{:S(2)}) collective-permute-start(bf16[16,128,256]{2,1,0:T(8,128)(2,1)S(1)} %constant_dynamic-update-slice_fusion), channel_id=1, source_target_pairs={{0,2},{1,3},{2,0},{3,1},{4,6},{5,7},{6,4},{7,5},{8,10},{9,11},{10,... | collective-permute-start | bytes 3145736 | tf_op jit(solution)/shard_map/ppermute | solution.py:35
  30.4 0.7 %copy-start.4 = (s32[256]{0:T(256)S(1)}, s32[256]{0:T(256)}, u32[]{:S(2)}) copy-start(s32[256]{0:T(256)} %param.9) | copy-start | bytes 3076
  31.1 0.7 %copy-start.5 = (s32[32]{0:T(128)S(1)}, s32[32]{0:T(128)}, u32[]{:S(2)}) copy-start(s32[32]{0:T(128)} %param.8) | copy-start | bytes 388

commit v2 on v1

--- a/solution.py
+++ b/solution.py
@@ -12,6 +12,7 @@
 
 
 NEG = -1e30
+LOG2_E = 1.4426950408889634
 
 ORDER_CORE0 = (4, 3, 2, 0)
 ORDER_CORE1 = (0, 2, 4, 3)
@@ -102,8 +103,8 @@
                     scores = jnp.where(visible, scores, NEG)
                 old_max = m_ref[...]
                 new_max = jnp.maximum(old_max, jnp.max(scores, axis=0, keepdims=True))
-                rescale = jnp.exp((old_max - new_max) * scale)
-                weights = jnp.exp((scores - new_max) * scale)
+                rescale = jnp.exp2((old_max - new_max) * scale)
+                weights = jnp.exp2((scores - new_max) * scale)
                 if masked:
                     weights = jnp.where(visible, weights, 0.0)
                 sums = jnp.sum(weights, axis=0, keepdims=True)
@@ -208,7 +209,7 @@
         last = index == len(pieces) - 1
         share = piece.shape[0] / n_spans
         kernel = functools.partial(
-            attend_kernel, heads=heads, span_len=span_len, scale=HEAD_DIM ** (-0.5),
+            attend_kernel, heads=heads, span_len=span_len, scale=HEAD_DIM ** (-0.5) * LOG2_E,
             base=base, first=first, last=last, n_local=n_local,
         )
         cost = pl.CostEstimate(

time: 57 us -> 56.4 us (0.989)
  the two profiles are of different devices: /device:TPU:16 before, /device:TPU:18 now
where the time goes in v2:
time: 56.4 us; the launch traced here: 56.1 us
  Pallas kernels  22.7 us (40%)
  waiting for transfers between devices  22.2 us (39%)
  starting transfers between devices  4.76 us (8%)
  local copies, waits for them, and re-layouts  4.44 us (8%)
  other arithmetic  1.9 us (3%)
    pallas_call x3, Pallas kernels, attend_all(): pl.pallas_call(kernel, in_specs=in_specs, out_specs=[vmem] * len(out_shap...  22.7 us
    ppermute x4, waiting for transfers between devices, doubling_gather(): other = lax.ppermute(held, ('ctx', 'head'), pairs)  22.2 us
    ppermute x4, starting transfers between devices, doubling_gather(): other = lax.ppermute(held, ('ctx', 'head'), pairs)  4.76 us
    unnamed x17, local copies, waits for them, and re-layouts  2.93 us
  transfers between devices with their start and end apart: 5, of which 4 were waited for; matrix products, arithmetic and copies ran while one was open for 6% of the time, Pallas kernels for 21%

profile of v2, /device:TPU:18, one launch (start us, length us, event | category | flops | bytes accessed | tf_op | source)
XLA Modules:
  0.0 56.1 jit_solution(13507559287996356737)
XLA Ops:
  0.0 0.0 copy-start.3
  0.0 0.9 %copy.9 = bf16[128,128]{0,1:T(8,128)(2,1)S(1)} copy(bf16[128,128]{1,0:T(8,128)(2,1)} %param.7) | data formatting | bytes 65536 | tf_op args[2]
  0.9 0.0 copy-done.3
  0.9 0.4 collective-permute-start
  1.3 4.9 %collective-permute-done = bf16[1,128,256]{2,1,0:T(8,128)(2,1)S(1)} collective-permute-done((bf16[1,128,256]{2,1,0:T(8,128)(2,1)S(1)}, bf16[1,128,256]{2,1,0:T(8,128)(2,1)S(1)}, u32[]{:S(2)}, u32[]{:S(2)}) %collective-permute-start) | collective-permute-done | bytes 65568 | tf_op jit(solution)/shard_map/ppermute | solution.py:31
  6.2 2.2 %collective-permute-start.1 = (bf16[2,128,256]{2,1,0:T(8,128)(2,1)S(1)}, bf16[2,128,256]{2,1,0:T(8,128)(2,1)S(1)}, u32[]{:S(2)}, u32[]{:S(2)}) collective-permute-start(bf16[2,128,256]{2,1,0:T(8,128)(2,1)S(1)} %pad_maximum_fusion.2), channel_id=1, source_target_pairs={{0,8},{1,9},{2,6},{3,7},{4,12},{5,13},{6,2},{7,3},{8,0},{9,1},{10,... | collective-permute-start | bytes 393224 | tf_op jit(solution)/shard_map/ppermute | solution.py:31
  8.4 3.9 %collective-permute-done.1 = bf16[2,128,256]{2,1,0:T(8,128)(2,1)S(1)} collective-permute-done((bf16[2,128,256]{2,1,0:T(8,128)(2,1)S(1)}, bf16[2,128,256]{2,1,0:T(8,128)(2,1)S(1)}, u32[]{:S(2)}, u32[]{:S(2)}) %collective-permute-start.1) | collective-permute-done | bytes 131104 | tf_op jit(solution)/shard_map/ppermute | solution.py:31
  12.3 1.6 %collective-permute-start.2 = (bf16[4,128,256]{2,1,0:T(8,128)(2,1)S(1)}, bf16[4,128,256]{2,1,0:T(8,128)(2,1)S(1)}, u32[]{:S(2)}, u32[]{:S(2)}) collective-permute-start(bf16[4,128,256]{2,1,0:T(8,128)(2,1)S(1)} %pad_maximum_fusion.1), channel_id=1, source_target_pairs={{0,4},{1,5},{2,18},{3,19},{4,0},{5,1},{6,22},{7,23},{8,12},{9,13},... | collective-permute-start | bytes 786440 | tf_op jit(solution)/shard_map/ppermute | solution.py:31
  13.9 4.9 %collective-permute-done.2 = bf16[4,128,256]{2,1,0:T(8,128)(2,1)S(1)} collective-permute-done((bf16[4,128,256]{2,1,0:T(8,128)(2,1)S(1)}, bf16[4,128,256]{2,1,0:T(8,128)(2,1)S(1)}, u32[]{:S(2)}, u32[]{:S(2)}) %collective-permute-start.2) | collective-permute-done | bytes 262176 | tf_op jit(solution)/shard_map/ppermute | solution.py:31
  18.8 0.0 copy-start.2
  18.8 0.6 %collective-permute-start.3 = (bf16[8,128,256]{2,1,0:T(8,128)(2,1)S(1)}, bf16[8,128,256]{2,1,0:T(8,128)(2,1)S(1)}, u32[]{:S(2)}, u32[]{:S(2)}) collective-permute-start(bf16[8,128,256]{2,1,0:T(8,128)(2,1)S(1)} %pad_maximum_fusion.kv_ref), channel_id=1, source_target_pairs={{0,1},{1,0},{2,10},{3,11},{4,5},{5,4},{6,14},{7,15},{8,9},{9,8},{1... | collective-permute-start | bytes 1572872 | tf_op jit(solution)/shard_map/ppermute | solution.py:31
  19.4 0.0 copy-start.1
  19.4 8.6 %collective-permute-done.3.kv_ref = bf16[8,128,256]{2,1,0:T(8,128)(2,1)S(1)} collective-permute-done((bf16[8,128,256]{2,1,0:T(8,128)(2,1)S(1)}, bf16[8,128,256]{2,1,0:T(8,128)(2,1)S(1)}, u32[]{:S(2)}, u32[]{:S(2)}) %collective-permute-start.3) | collective-permute-done | bytes 524320 | tf_op jit(solution)/shard_map/ppermute | solution.py:31
  28.0 0.0 copy-start
  28.1 0.0 copy-done.2
  28.1 0.7 %copy-done = bf16[8,128,256]{2,1,0:T(8,128)(2,1)} copy-done((bf16[8,128,256]{2,1,0:T(8,128)(2,1)}, bf16[8,128,256]{2,1,0:T(8,128)(2,1)S(1)}, u32[]{:S(2)}) %copy-start) | copy-done | bytes 524312
  28.8 0.0 collective-permute-start.4
  28.8 0.0 copy-done.1
  28.8 0.1 copy.10
  28.9 0.5 copy.8
  29.4 1.0 %reshape.167.qt_ref = bf16[2,128,1024]{2,1,0:T(8,128)(2,1)} reshape(bf16[2,128,8,128]{3,2,1,0:T(8,128)(2,1)S(1)} %bitcast.31) | data formatting | bytes 1048576 | tf_op jit(solution)/shard_map/reshape | solution.py:194
  30.4 0.7 %copy-done.4 = s32[256]{0:T(256)S(1)} copy-done((s32[256]{0:T(256)S(1)}, s32[256]{0:T(256)}, u32[]{:S(2)}) %copy-start.4) | copy-done | bytes 1048
  31.1 0.1 bitcast_reduce_fusion.1
  31.2 0.5 copy-done.5
  31.7 0.2 fusion
  31.9 0.6 %pad_add_fusion.info_ref = s32[3,2]{1,0:T(4,128)} fusion(s32[1,2]{1,0:T(1,128)S(1)} %get-tuple-element.23, s32[1,2]{1,0:T(1,128)S(1)} %get-tuple-element.24, s32[1,2]{1,0:T(1,128)S(1)} %bitcast.45), kind=kLoop, calls=%fused_computation.12 | loop fusion | flops 12 | bytes 48 | tf_op jit(solution)/shard_map/stack | solution.py:188
  32.5 0.1 select_reduce_fusion.1
  32.7 0.8 %select_reduce_fusion.slot_ref = s32[32]{0:T(128)} fusion(s32[32]{0:T(128)S(1)} %compare_select_fusion, s32[32]{0:T(128)S(1)} %select_reduce_fusion.1), kind=kLoop, calls=%fused_computation.4 | loop fusion | flops 3040 | bytes 384 | tf_op jit(solution)/shard_map/reduce_sum | solution.py:177
  33.4 5.3 %shard_map.55 = (f32[2,1,1024]{2,1,0:T(1,128)}, f32[2,1,1024]{2,1,0:T(1,128)}, f32[2,128,1024]{2,1,0:T(8,128)}) custom-call(s32[3,2]{1,0:T(4,128)} %pad_add_fusion.info_ref, s32[32]{0:T(128)} %select_reduce_fusion.slot_ref, bf16[2,128,1024]{2,1,0:T(8,128)(2,1)} %reshape.167.qt_ref, bf16[8,128,256]{2,1,0:T(8,128)(2,1)} %copy-done.2, s32[2,1,128]{2,1,0:T(1,128)} %bitcast.42), custom_call_target="tpu_custom_call" | custom-call | flops 570425344 | bytes 1572864 | tf_op jit(solution)/shard_map/pallas_call | solution.py:226
  38.8 6.5 %shard_map.56 = (f32[2,1,1024]{2,1,0:T(1,128)}, f32[2,1,1024]{2,1,0:T(1,128)}, f32[2,128,1024]{2,1,0:T(8,128)}) custom-call(s32[3,2]{1,0:T(4,128)} %pad_add_fusion.info_ref, s32[32]{0:T(128)} %select_reduce_fusion.slot_ref, bf16[2,128,1024]{2,1,0:T(8,128)(2,1)} %reshape.167.qt_ref, bf16[8,128,256]{2,1,0:T(8,128)(2,1)} %copy-done, s32[2,1,128]{2,1,0:T(1,128)} %bitcast.43, ...), custom_call_target="tpu_custom_call" | custom-call | flops 570425344 | bytes 1572864 | tf_op jit(solution)/shard_map/pallas_call | solution.py:226
  45.2 0.0 collective-permute-done.4.kv_ref
  45.2 10.9 %shard_map.57 = (f32[2,1,1024]{2,1,0:T(1,128)}, f32[2,1,1024]{2,1,0:T(1,128)}, f32[2,128,1024]{2,1,0:T(8,128)}, bf16[256,1024]{1,0:T(8,128)(2,1)}) custom-call(s32[3,2]{1,0:T(4,128)} %pad_add_fusion.info_ref, s32[32]{0:T(128)} %select_reduce_fusion.slot_ref, bf16[2,128,1024]{2,1,0:T(8,128)(2,1)} %reshape.167.qt_ref, ...), custom_call_target="tpu_custom_call" | custom-call | flops 1140850688 | bytes 2097152 | tf_op jit(solution)/shard_map/pallas_call | solution.py:226
  (13 shorter events, 0.2 us)
Async XLA Ops:
  0.0 0.9 %copy-start.3 = (bf16[128,128]{1,0:T(8,128)(2,1)S(1)}, bf16[128,128]{1,0:T(8,128)(2,1)}, u32[]{:S(2)}) copy-start(bf16[128,128]{1,0:T(8,128)(2,1)} %param.6) | copy-start | bytes 98308
  0.9 5.3 %collective-permute-start = (bf16[1,128,256]{2,1,0:T(8,128)(2,1)S(1)}, bf16[1,128,256]{2,1,0:T(8,128)(2,1)S(1)}, u32[]{:S(2)}, u32[]{:S(2)}) collective-permute-start(bf16[1,128,256]{2,1,0:T(8,128)(2,1)S(1)} %get-tuple-element.21), channel_id=1, source_target_pairs={{0,16},{1,17},{2,3},{3,2},{4,20},{5,21},{6,7},{7,6},{8,24},{9,25},... | collective-permute-start | bytes 196616 | tf_op jit(solution)/shard_map/ppermute | solution.py:31
  6.2 6.1 %collective-permute-start.1 = (bf16[2,128,256]{2,1,0:T(8,128)(2,1)S(1)}, bf16[2,128,256]{2,1,0:T(8,128)(2,1)S(1)}, u32[]{:S(2)}, u32[]{:S(2)}) collective-permute-start(bf16[2,128,256]{2,1,0:T(8,128)(2,1)S(1)} %pad_maximum_fusion.2), channel_id=1, source_target_pairs={{0,8},{1,9},{2,6},{3,7},{4,12},{5,13},{6,2},{7,3},{8,0},{9,1},{10,... | collective-permute-start | bytes 393224 | tf_op jit(solution)/shard_map/ppermute | solution.py:31
  12.3 6.4 %collective-permute-start.2 = (bf16[4,128,256]{2,1,0:T(8,128)(2,1)S(1)}, bf16[4,128,256]{2,1,0:T(8,128)(2,1)S(1)}, u32[]{:S(2)}, u32[]{:S(2)}) collective-permute-start(bf16[4,128,256]{2,1,0:T(8,128)(2,1)S(1)} %pad_maximum_fusion.1), channel_id=1, source_target_pairs={{0,4},{1,5},{2,18},{3,19},{4,0},{5,1},{6,22},{7,23},{8,12},{9,13},... | collective-permute-start | bytes 786440 | tf_op jit(solution)/shard_map/ppermute | solution.py:31
  18.8 9.3 %copy-start.2 = (bf16[8,128,256]{2,1,0:T(8,128)(2,1)}, bf16[8,128,256]{2,1,0:T(8,128)(2,1)S(1)}, u32[]{:S(2)}) copy-start(bf16[8,128,256]{2,1,0:T(8,128)(2,1)S(1)} %pad_maximum_fusion.kv_ref) | copy-start | bytes 1572868
  18.8 9.2 %collective-permute-start.3 = (bf16[8,128,256]{2,1,0:T(8,128)(2,1)S(1)}, bf16[8,128,256]{2,1,0:T(8,128)(2,1)S(1)}, u32[]{:S(2)}, u32[]{:S(2)}) collective-permute-start(bf16[8,128,256]{2,1,0:T(8,128)(2,1)S(1)} %pad_maximum_fusion.kv_ref), channel_id=1, source_target_pairs={{0,1},{1,0},{2,10},{3,11},{4,5},{5,4},{6,14},{7,15},{8,9},{9,8},{1... | collective-permute-start | bytes 1572872 | tf_op jit(solution)/shard_map/ppermute | solution.py:31
  19.4 9.4 %copy-start.1 = (bf16[256,1024]{1,0:T(8,128)(2,1)S(1)}, bf16[256,1024]{1,0:T(8,128)(2,1)}, u32[]{:S(2)}) copy-start(bf16[256,1024]{1,0:T(8,128)(2,1)} %param.5) | copy-start | bytes 1572868
  28.0 0.8 %copy-start = (bf16[8,128,256]{2,1,0:T(8,128)(2,1)}, bf16[8,128,256]{2,1,0:T(8,128)(2,1)S(1)}, u32[]{:S(2)}) copy-start(bf16[8,128,256]{2,1,0:T(8,128)(2,1)S(1)} %collective-permute-done.3.kv_ref) | copy-start | bytes 1572868
  28.8 16.4 %collective-permute-start.4 = (bf16[16,128,256]{2,1,0:T(8,128)(2,1)S(1)}, bf16[16,128,256]{2,1,0:T(8,128)(2,1)}, u32[]{:S(2)}, u32[]{:S(2)}) collective-permute-start(bf16[16,128,256]{2,1,0:T(8,128)(2,1)S(1)} %constant_dynamic-update-slice_fusion), channel_id=1, source_target_pairs={{0,2},{1,3},{2,0},{3,1},{4,6},{5,7},{6,4},{7,5},{8,10},{9,11},{10,... | collective-permute-start | bytes 3145736 | tf_op jit(solution)/shard_map/ppermute | solution.py:36
  30.4 0.7 %copy-start.4 = (s32[256]{0:T(256)S(1)}, s32[256]{0:T(256)}, u32[]{:S(2)}) copy-start(s32[256]{0:T(256)} %param.9) | copy-start | bytes 3076
  31.1 0.7 %copy-start.5 = (s32[32]{0:T(128)S(1)}, s32[32]{0:T(128)}, u32[]{:S(2)}) copy-start(s32[32]{0:T(128)} %param.8) | copy-start | bytes 388

commit v3 on v2

--- a/solution.py
+++ b/solution.py
@@ -32,9 +32,11 @@
         if step == len(ORDER_CORE0) - 1:
             pieces.append(held)
             pieces.append(other)
-        held = jnp.concatenate([held, other], axis=0)
+            held = (held, other)
+        else:
+            held = jnp.concatenate([held, other], axis=0)
     other = lax.ppermute(held, ("ctx", "head"), [(k, k ^ (1 << CORE_BIT)) for k in range(n_dev)])
-    pieces.append(other)
+    pieces.append(tuple(other))
 
     def source_mask(order, j):
         mask = 0
@@ -54,15 +56,28 @@
     return pieces, source
 
 
-def attend_kernel(info_ref, slot_ref, qt_ref, kv_ref, doc_ref, *rest,
-                  heads, span_len, scale, base, first, last, n_local):
+def attend_kernel(info_ref, slot_ref, qt_ref, *rest,
+                  heads, span_len, scale, base, first, last, n_local, n_kv):
     rest = list(rest)
+    kv_refs = rest[:n_kv]
+    doc_ref = rest[n_kv]
+    rest = rest[n_kv + 1:]
     if not first:
         im_all, il_all, iacc_all = rest[:3]
         rest = rest[3:]
     m_all, l_all, acc_all = rest[:3]
     o_ref = rest[3] if last else None
-    count = kv_ref.shape[0]
+    count = sum(r.shape[0] for r in kv_refs)
+
+    def load_kv(b):
+        kv = kv_refs[0][jnp.minimum(b, kv_refs[0].shape[0] - 1)]
+        offset = kv_refs[0].shape[0]
+        for r in kv_refs[1:]:
+            here = r[jnp.clip(b - offset, 0, r.shape[0] - 1)]
+            kv = jnp.where(b >= offset, here, kv)
+            offset += r.shape[0]
+        return kv
+
     rows = heads * span_len
     cols = lax.broadcasted_iota(jnp.int32, (1, rows), 1)
 
@@ -93,7 +108,7 @@
 
             @pl.when((b >= 0) & (b < count))
             def _():
-                kv = kv_ref[b]
+                kv = load_kv(b)
                 keys = kv[:, :HEAD_DIM]
                 vals_t = kv[:, HEAD_DIM:]
                 scores = jnp.dot(keys, qt_ref_j[...], preferred_element_type=jnp.float32)
@@ -131,7 +146,7 @@
             for h in range(heads):
                 o_ref[j * span_len:(j + 1) * span_len, h * HEAD_DIM:(h + 1) * HEAD_DIM] = out_t[
                     :, h * span_len:(h + 1) * span_len
-                ].T.astype(o_ref.dtype)
+                ].astype(o_ref.dtype).T
 
 
 def span_blocks(keys, vals, span_len):
@@ -207,18 +222,20 @@
     for index, piece in enumerate(pieces):
         first = index == 0
         last = index == len(pieces) - 1
-        share = piece.shape[0] / n_spans
+        piece = tuple(piece) if isinstance(piece, tuple) else (piece,)
+        n_blocks = sum(x.shape[0] for x in piece)
+        share = n_blocks / n_spans
         kernel = functools.partial(
             attend_kernel, heads=heads, span_len=span_len, scale=HEAD_DIM ** (-0.5) * LOG2_E,
-            base=base, first=first, last=last, n_local=n_local,
+            base=base, first=first, last=last, n_local=n_local, n_kv=len(piece),
         )
         cost = pl.CostEstimate(
             flops=int(4 * rows * span_len * HEAD_DIM * blocks_est * share),
             transcendentals=int(rows * span_len * blocks_est * share),
-            bytes_accessed=2 * queries.size * 2 + piece.size * 2,
+            bytes_accessed=2 * queries.size * 2 + n_blocks * span_len * 4 * HEAD_DIM,
         )
-        operands = [info, where_held, q_t, piece, doc_rows]
-        in_specs = [smem, smem, vmem, vmem, vmem]
+        operands = [info, where_held, q_t, *piece, doc_rows]
+        in_specs = [smem, smem, vmem] + [vmem] * len(piece) + [vmem]
         if not first:
             operands = operands + list(state)
             in_specs = in_specs + [vmem] * 3
@@ -230,7 +247,7 @@
             out_shape=out_shapes,
             cost_estimate=cost,
         )(*operands)
-        base += piece.shape[0]
+        base += n_blocks
         if last:
             return result[3]
         state = result[:3]

time: 56.4 us -> 53.6 us (0.950)
  the two profiles are of different devices: /device:TPU:18 before, /device:TPU:16 now
where the time goes in v3:
time: 53.6 us; the launch traced here: 53.4 us
  Pallas kernels  22.7 us (42%)
  waiting for transfers between devices  19.1 us (36%)
  starting transfers between devices  5.46 us (10%)
  local copies, waits for them, and re-layouts  3.98 us (7%)
  other arithmetic  1.99 us (4%)
    pallas_call x3, Pallas kernels, attend_all(): pl.pallas_call(kernel, in_specs=in_specs, out_specs=[vmem] * len(out_shap...  22.7 us
    ppermute x4, waiting for transfers between devices, doubling_gather(): other = lax.ppermute(held, ('ctx', 'head'), pairs)  19.1 us
    ppermute x4, starting transfers between devices, doubling_gather(): other = lax.ppermute(held, ('ctx', 'head'), pairs)  5.38 us
    unnamed x18, local copies, waits for them, and re-layouts  2.51 us
  transfers between devices with their start and end apart: 6, of which 4 were waited for; matrix products, arithmetic and copies ran while one was open for 7% of the time, Pallas kernels for 22%

profile of v3, /device:TPU:16, one launch (start us, length us, event | category | flops | bytes accessed | tf_op | source)
XLA Modules:
  0.0 53.4 jit_solution(14585071961519176273)
XLA Ops:
  0.0 0.9 %copy.9 = bf16[128,128]{0,1:T(8,128)(2,1)S(1)} copy(bf16[128,128]{1,0:T(8,128)(2,1)} %param.7) | data formatting | bytes 65536 | tf_op args[2]
  0.9 0.0 copy-done.3
  1.0 0.1 collective-permute-start
  1.0 5.2 %collective-permute-done = bf16[1,128,256]{2,1,0:T(8,128)(2,1)S(1)} collective-permute-done((bf16[1,128,256]{2,1,0:T(8,128)(2,1)S(1)}, bf16[1,128,256]{2,1,0:T(8,128)(2,1)S(1)}, u32[]{:S(2)}, u32[]{:S(2)}) %collective-permute-start) | collective-permute-done | bytes 65568 | tf_op jit(solution)/shard_map/ppermute | solution.py:31
  6.3 2.2 %collective-permute-start.1 = (bf16[2,128,256]{2,1,0:T(8,128)(2,1)S(1)}, bf16[2,128,256]{2,1,0:T(8,128)(2,1)S(1)}, u32[]{:S(2)}, u32[]{:S(2)}) collective-permute-start(bf16[2,128,256]{2,1,0:T(8,128)(2,1)S(1)} %pad_maximum_fusion.2), channel_id=1, source_target_pairs={{0,8},{1,9},{2,6},{3,7},{4,12},{5,13},{6,2},{7,3},{8,0},{9,1},{10,... | collective-permute-start | bytes 393224 | tf_op jit(solution)/shard_map/ppermute | solution.py:31
  8.4 3.9 %collective-permute-done.1 = bf16[2,128,256]{2,1,0:T(8,128)(2,1)S(1)} collective-permute-done((bf16[2,128,256]{2,1,0:T(8,128)(2,1)S(1)}, bf16[2,128,256]{2,1,0:T(8,128)(2,1)S(1)}, u32[]{:S(2)}, u32[]{:S(2)}) %collective-permute-start.1) | collective-permute-done | bytes 131104 | tf_op jit(solution)/shard_map/ppermute | solution.py:31
  12.3 1.6 %collective-permute-start.2 = (bf16[4,128,256]{2,1,0:T(8,128)(2,1)S(1)}, bf16[4,128,256]{2,1,0:T(8,128)(2,1)S(1)}, u32[]{:S(2)}, u32[]{:S(2)}) collective-permute-start(bf16[4,128,256]{2,1,0:T(8,128)(2,1)S(1)} %pad_maximum_fusion.1), channel_id=1, source_target_pairs={{0,4},{1,5},{2,18},{3,19},{4,0},{5,1},{6,22},{7,23},{8,12},{9,13},... | collective-permute-start | bytes 786440 | tf_op jit(solution)/shard_map/ppermute | solution.py:31
  13.9 0.0 copy-done.1
  13.9 0.1 copy.10
  14.0 0.5 copy.8
  14.5 1.0 %reshape.167.qt_ref = bf16[2,128,1024]{2,1,0:T(8,128)(2,1)} reshape(bf16[2,128,8,128]{3,2,1,0:T(8,128)(2,1)S(1)} %bitcast.31) | data formatting | bytes 1048576 | tf_op jit(solution)/shard_map/reshape | solution.py:209
  15.5 3.3 %collective-permute-done.2 = bf16[4,128,256]{2,1,0:T(8,128)(2,1)S(1)} collective-permute-done((bf16[4,128,256]{2,1,0:T(8,128)(2,1)S(1)}, bf16[4,128,256]{2,1,0:T(8,128)(2,1)S(1)}, u32[]{:S(2)}, u32[]{:S(2)}) %collective-permute-start.2) | collective-permute-done | bytes 262176 | tf_op jit(solution)/shard_map/ppermute | solution.py:31
  18.8 0.0 copy-start.2
  18.8 0.0 copy-start.4
  18.8 1.6 %collective-permute-start.4 = (bf16[8,128,256]{2,1,0:T(8,128)(2,1)S(1)}, bf16[8,128,256]{2,1,0:T(8,128)(2,1)S(1)}, u32[]{:S(2)}, u32[]{:S(2)}) collective-permute-start(bf16[8,128,256]{2,1,0:T(8,128)(2,1)S(1)} %pad_maximum_fusion.rest_0_), channel_id=1, source_target_pairs={{0,1},{1,0},{2,10},{3,11},{4,5},{5,4},{6,14},{7,15},{8,9},{9,8},{1... | collective-permute-start | bytes 1572872 | tf_op jit(solution)/shard_map/ppermute | solution.py:31
  20.4 0.0 copy-done.4
  20.4 0.1 bitcast_reduce_fusion.1
  20.6 0.5 copy-done.7
  21.1 0.2 fusion
  21.3 0.1 collective-permute-start.3
  21.3 6.8 %collective-permute-done.4.rest_0_ = bf16[8,128,256]{2,1,0:T(8,128)(2,1)S(1)} collective-permute-done((bf16[8,128,256]{2,1,0:T(8,128)(2,1)S(1)}, bf16[8,128,256]{2,1,0:T(8,128)(2,1)S(1)}, u32[]{:S(2)}, u32[]{:S(2)}) %collective-permute-start.4) | collective-permute-done | bytes 524320 | tf_op jit(solution)/shard_map/ppermute | solution.py:31
  28.1 0.0 collective-permute-start.5
  28.1 0.7 %pad_add_fusion.info_ref = s32[3,2]{1,0:T(4,128)} fusion(s32[1,2]{1,0:T(1,128)S(1)} %get-tuple-element.21, s32[1,2]{1,0:T(1,128)S(1)} %get-tuple-element.22, s32[1,2]{1,0:T(1,128)S(1)} %bitcast.45), kind=kLoop, calls=%fused_computation.7 | loop fusion | flops 12 | bytes 48 | tf_op jit(solution)/shard_map/stack | solution.py:203
  28.8 0.1 select_reduce_fusion.1
  28.9 0.8 %select_reduce_fusion.slot_ref = s32[32]{0:T(128)} fusion(s32[32]{0:T(128)S(1)} %compare_select_fusion, s32[32]{0:T(128)S(1)} %select_reduce_fusion.1), kind=kLoop, calls=%fused_computation.4 | loop fusion | flops 3040 | bytes 384 | tf_op jit(solution)/shard_map/reduce_sum | solution.py:192
  29.7 6.0 %shard_map.55 = (f32[2,1,1024]{2,1,0:T(1,128)}, f32[2,1,1024]{2,1,0:T(1,128)}, f32[2,128,1024]{2,1,0:T(8,128)}) custom-call(s32[3,2]{1,0:T(4,128)} %pad_add_fusion.info_ref, s32[32]{0:T(128)} %select_reduce_fusion.slot_ref, bf16[2,128,1024]{2,1,0:T(8,128)(2,1)} %reshape.167.qt_ref, bf16[8,128,256]{2,1,0:T(8,128)(2,1)} %copy-done.2, s32[2,1,128]{2,1,0:T(1,128)} %bitcast.42), custom_call_target="tpu_custom_call" | custom-call | flops 570425344 | bytes 1572864 | tf_op jit(solution)/shard_map/pallas_call | solution.py:243
  35.7 5.7 %shard_map.56 = (f32[2,1,1024]{2,1,0:T(1,128)}, f32[2,1,1024]{2,1,0:T(1,128)}, f32[2,128,1024]{2,1,0:T(8,128)}) custom-call(s32[3,2]{1,0:T(4,128)} %pad_add_fusion.info_ref, s32[32]{0:T(128)} %select_reduce_fusion.slot_ref, bf16[2,128,1024]{2,1,0:T(8,128)(2,1)} %reshape.167.qt_ref, bf16[8,128,256]{2,1,0:T(8,128)(2,1)} %copy-done, s32[2,1,128]{2,1,0:T(1,128)} %bitcast.43, ...), custom_call_target="tpu_custom_call" | custom-call | flops 570425344 | bytes 1572864 | tf_op jit(solution)/shard_map/pallas_call | solution.py:243
  41.5 0.0 collective-permute-done.3.rest_0_
  41.5 0.0 collective-permute-done.5.rest_1_
  41.5 0.8 %copy-done.5 = bf16[8,128,256]{2,1,0:T(8,128)(2,1)} copy-done((bf16[8,128,256]{2,1,0:T(8,128)(2,1)}, bf16[8,128,256]{2,1,0:T(8,128)(2,1)S(1)}, u32[]{:S(2)}) %copy-start.5) | copy-done | bytes 524312
  42.3 0.2 copy-done.6
  42.4 11.0 %shard_map.57 = (f32[2,1,1024]{2,1,0:T(1,128)}, f32[2,1,1024]{2,1,0:T(1,128)}, f32[2,128,1024]{2,1,0:T(8,128)}, bf16[256,1024]{1,0:T(8,128)(2,1)}) custom-call(s32[3,2]{1,0:T(4,128)} %pad_add_fusion.info_ref, s32[32]{0:T(128)} %select_reduce_fusion.slot_ref, bf16[2,128,1024]{2,1,0:T(8,128)(2,1)} %reshape.167.qt_ref, bf16[8,128,256]{2,1,0:T(8,128)(2,1)} %copy-done.5, ...), custom_call_target="tpu_custom_call" | custom-call | flops 1140850688 | bytes 2097152 | tf_op jit(solution)/shard_map/pallas_call | solution.py:243
  (15 shorter events, 0.1 us)
Async XLA Ops:
  0.0 0.9 %copy-start.3 = (bf16[128,128]{1,0:T(8,128)(2,1)S(1)}, bf16[128,128]{1,0:T(8,128)(2,1)}, u32[]{:S(2)}) copy-start(bf16[128,128]{1,0:T(8,128)(2,1)} %param.6) | copy-start | bytes 98308
  0.0 13.9 %copy-start.1 = (bf16[256,1024]{1,0:T(8,128)(2,1)S(1)}, bf16[256,1024]{1,0:T(8,128)(2,1)}, u32[]{:S(2)}) copy-start(bf16[256,1024]{1,0:T(8,128)(2,1)} %param.5) | copy-start | bytes 1572868
  1.0 5.3 %collective-permute-start = (bf16[1,128,256]{2,1,0:T(8,128)(2,1)S(1)}, bf16[1,128,256]{2,1,0:T(8,128)(2,1)S(1)}, u32[]{:S(2)}, u32[]{:S(2)}) collective-permute-start(bf16[1,128,256]{2,1,0:T(8,128)(2,1)S(1)} %pad_maximum_fusion.3), channel_id=1, source_target_pairs={{0,16},{1,17},{2,3},{3,2},{4,20},{5,21},{6,7},{7,6},{8,24},{9,25},... | collective-permute-start | bytes 196616 | tf_op jit(solution)/shard_map/ppermute | solution.py:31
  6.3 6.1 %collective-permute-start.1 = (bf16[2,128,256]{2,1,0:T(8,128)(2,1)S(1)}, bf16[2,128,256]{2,1,0:T(8,128)(2,1)S(1)}, u32[]{:S(2)}, u32[]{:S(2)}) collective-permute-start(bf16[2,128,256]{2,1,0:T(8,128)(2,1)S(1)} %pad_maximum_fusion.2), channel_id=1, source_target_pairs={{0,8},{1,9},{2,6},{3,7},{4,12},{5,13},{6,2},{7,3},{8,0},{9,1},{10,... | collective-permute-start | bytes 393224 | tf_op jit(solution)/shard_map/ppermute | solution.py:31
  12.3 6.4 %collective-permute-start.2 = (bf16[4,128,256]{2,1,0:T(8,128)(2,1)S(1)}, bf16[4,128,256]{2,1,0:T(8,128)(2,1)S(1)}, u32[]{:S(2)}, u32[]{:S(2)}) collective-permute-start(bf16[4,128,256]{2,1,0:T(8,128)(2,1)S(1)} %pad_maximum_fusion.1), channel_id=1, source_target_pairs={{0,4},{1,5},{2,18},{3,19},{4,0},{5,1},{6,22},{7,23},{8,12},{9,13},... | collective-permute-start | bytes 786440 | tf_op jit(solution)/shard_map/ppermute | solution.py:31
  18.8 10.8 %copy-start.2 = (bf16[8,128,256]{2,1,0:T(8,128)(2,1)}, bf16[8,128,256]{2,1,0:T(8,128)(2,1)S(1)}, u32[]{:S(2)}) copy-start(bf16[8,128,256]{2,1,0:T(8,128)(2,1)S(1)} %pad_maximum_fusion.rest_0_) | copy-start | bytes 1572868
  18.8 1.6 %copy-start.4 = (s32[256]{0:T(256)S(1)}, s32[256]{0:T(256)}, u32[]{:S(2)}) copy-start(s32[256]{0:T(256)} %param.9) | copy-start | bytes 3076
  18.8 9.2 %collective-permute-start.4 = (bf16[8,128,256]{2,1,0:T(8,128)(2,1)S(1)}, bf16[8,128,256]{2,1,0:T(8,128)(2,1)S(1)}, u32[]{:S(2)}, u32[]{:S(2)}) collective-permute-start(bf16[8,128,256]{2,1,0:T(8,128)(2,1)S(1)} %pad_maximum_fusion.rest_0_), channel_id=1, source_target_pairs={{0,1},{1,0},{2,10},{3,11},{4,5},{5,4},{6,14},{7,15},{8,9},{9,8},{1... | collective-permute-start | bytes 1572872 | tf_op jit(solution)/shard_map/ppermute | solution.py:31
  20.4 0.7 %copy-start.7 = (s32[32]{0:T(128)S(1)}, s32[32]{0:T(128)}, u32[]{:S(2)}) copy-start(s32[32]{0:T(128)} %param.8) | copy-start | bytes 388
  21.3 20.2 %collective-permute-start.3 = (bf16[8,128,256]{2,1,0:T(8,128)(2,1)S(1)}, bf16[8,128,256]{2,1,0:T(8,128)(2,1)S(1)}, u32[]{:S(2)}, u32[]{:S(2)}) collective-permute-start(bf16[8,128,256]{2,1,0:T(8,128)(2,1)S(1)} %pad_maximum_fusion.rest_0_), channel_id=1, source_target_pairs={{0,2},{1,3},{2,0},{3,1},{4,6},{5,7},{6,4},{7,5},{8,10},{9,11},{10,... | collective-permute-start | bytes 1572872 | tf_op jit(solution)/shard_map/ppermute | solution.py:38
  28.1 7.6 %copy-start = (bf16[8,128,256]{2,1,0:T(8,128)(2,1)}, bf16[8,128,256]{2,1,0:T(8,128)(2,1)S(1)}, u32[]{:S(2)}) copy-start(bf16[8,128,256]{2,1,0:T(8,128)(2,1)S(1)} %collective-permute-done.4.rest_0_) | copy-start | bytes 1572868
  28.1 13.4 %collective-permute-start.5 = (bf16[8,128,256]{2,1,0:T(8,128)(2,1)S(1)}, bf16[8,128,256]{2,1,0:T(8,128)(2,1)S(1)}, u32[]{:S(2)}, u32[]{:S(2)}) collective-permute-start(bf16[8,128,256]{2,1,0:T(8,128)(2,1)S(1)} %collective-permute-done.4.rest_0_), channel_id=1, source_target_pairs={{0,2},{1,3},{2,0},{3,1},{4,6},{5,7},{6,4},{7,5},{8,10},{9,11},{10,... | collective-permute-start | bytes 1572872 | tf_op jit(solution)/shard_map/ppermute | solution.py:38
  41.5 0.8 %copy-start.5 = (bf16[8,128,256]{2,1,0:T(8,128)(2,1)}, bf16[8,128,256]{2,1,0:T(8,128)(2,1)S(1)}, u32[]{:S(2)}) copy-start(bf16[8,128,256]{2,1,0:T(8,128)(2,1)S(1)} %collective-permute-done.3.rest_0_) | copy-start | bytes 1572868
  41.5 1.0 %copy-start.6 = (bf16[8,128,256]{2,1,0:T(8,128)(2,1)}, bf16[8,128,256]{2,1,0:T(8,128)(2,1)S(1)}, u32[]{:S(2)}) copy-start(bf16[8,128,256]{2,1,0:T(8,128)(2,1)S(1)} %collective-permute-done.5.rest_1_) | copy-start | bytes 1572868

commit v4 on v3

--- a/solution.py
+++ b/solution.py
@@ -12,6 +12,7 @@
 
 
 NEG = -1e30
+START_MAX = -1e29
 LOG2_E = 1.4426950408889634
 
 ORDER_CORE0 = (4, 3, 2, 0)
@@ -91,7 +92,7 @@
         qt_ref_j = qt_ref.at[j]
 
         if first:
-            m_ref[...] = jnp.full(m_ref.shape, NEG, jnp.float32)
+            m_ref[...] = jnp.full(m_ref.shape, START_MAX, jnp.float32)
             l_ref[...] = jnp.zeros(l_ref.shape, jnp.float32)
             acc_ref[...] = jnp.zeros(acc_ref.shape, jnp.float32)
         else:
@@ -120,8 +121,6 @@
                 new_max = jnp.maximum(old_max, jnp.max(scores, axis=0, keepdims=True))
                 rescale = jnp.exp2((old_max - new_max) * scale)
                 weights = jnp.exp2((scores - new_max) * scale)
-                if masked:
-                    weights = jnp.where(visible, weights, 0.0)
                 sums = jnp.sum(weights, axis=0, keepdims=True)
                 mixed = jnp.dot(vals_t, weights.astype(jnp.bfloat16), preferred_element_type=jnp.float32)
                 l_ref[...] = rescale * l_ref[...] + sums

time: 53.6 us -> 52.2 us (0.974)
  Pallas kernels: 22.7 us -> 21.4 us
    pallas_call x3, Pallas kernels: 22.7 us -> 21.4 us  [attend_all(): pl.pallas_call(kernel, in_specs=in_specs, out_specs=[vmem] * len(out_shap...]
  transfers between devices with their start and end apart: 6 -> 6, of which waited for: 4 -> 4; matrix products, arithmetic and copies ran while one was open for 7% -> 7% of each run, Pallas kernels for 22% -> 21%
where the time goes in v4:
time: 52.2 us; the launch traced here: 52 us
  Pallas kernels  21.4 us (41%)
  waiting for transfers between devices  19.1 us (37%)
  starting transfers between devices  5.46 us (10%)
  local copies, waits for them, and re-layouts  3.98 us (8%)
  other arithmetic  1.99 us (4%)
    pallas_call x3, Pallas kernels, attend_all(): pl.pallas_call(kernel, in_specs=in_specs, out_specs=[vmem] * len(out_shap...  21.4 us
    ppermute x4, waiting for transfers between devices, doubling_gather(): other = lax.ppermute(held, ('ctx', 'head'), pairs)  19.1 us
    ppermute x4, starting transfers between devices, doubling_gather(): other = lax.ppermute(held, ('ctx', 'head'), pairs)  5.38 us
    unnamed x18, local copies, waits for them, and re-layouts  2.51 us
  transfers between devices with their start and end apart: 6, of which 4 were waited for; matrix products, arithmetic and copies ran while one was open for 7% of the time, Pallas kernels for 21%

profile of v4, /device:TPU:16, one launch (start us, length us, event | category | flops | bytes accessed | tf_op | source)
XLA Modules:
  0.0 52.0 jit_solution(9905422687902851055)
XLA Ops:
  0.0 0.9 %copy.9 = bf16[128,128]{0,1:T(8,128)(2,1)S(1)} copy(bf16[128,128]{1,0:T(8,128)(2,1)} %param.7) | data formatting | bytes 65536 | tf_op args[2]
  0.9 0.0 copy-done.3
  1.0 0.1 collective-permute-start
  1.0 5.2 %collective-permute-done = bf16[1,128,256]{2,1,0:T(8,128)(2,1)S(1)} collective-permute-done((bf16[1,128,256]{2,1,0:T(8,128)(2,1)S(1)}, bf16[1,128,256]{2,1,0:T(8,128)(2,1)S(1)}, u32[]{:S(2)}, u32[]{:S(2)}) %collective-permute-start) | collective-permute-done | bytes 65568 | tf_op jit(solution)/shard_map/ppermute | solution.py:32
  6.3 2.2 %collective-permute-start.1 = (bf16[2,128,256]{2,1,0:T(8,128)(2,1)S(1)}, bf16[2,128,256]{2,1,0:T(8,128)(2,1)S(1)}, u32[]{:S(2)}, u32[]{:S(2)}) collective-permute-start(bf16[2,128,256]{2,1,0:T(8,128)(2,1)S(1)} %pad_maximum_fusion.2), channel_id=1, source_target_pairs={{0,8},{1,9},{2,6},{3,7},{4,12},{5,13},{6,2},{7,3},{8,0},{9,1},{10,... | collective-permute-start | bytes 393224 | tf_op jit(solution)/shard_map/ppermute | solution.py:32
  8.4 3.9 %collective-permute-done.1 = bf16[2,128,256]{2,1,0:T(8,128)(2,1)S(1)} collective-permute-done((bf16[2,128,256]{2,1,0:T(8,128)(2,1)S(1)}, bf16[2,128,256]{2,1,0:T(8,128)(2,1)S(1)}, u32[]{:S(2)}, u32[]{:S(2)}) %collective-permute-start.1) | collective-permute-done | bytes 131104 | tf_op jit(solution)/shard_map/ppermute | solution.py:32
  12.3 1.6 %collective-permute-start.2 = (bf16[4,128,256]{2,1,0:T(8,128)(2,1)S(1)}, bf16[4,128,256]{2,1,0:T(8,128)(2,1)S(1)}, u32[]{:S(2)}, u32[]{:S(2)}) collective-permute-start(bf16[4,128,256]{2,1,0:T(8,128)(2,1)S(1)} %pad_maximum_fusion.1), channel_id=1, source_target_pairs={{0,4},{1,5},{2,18},{3,19},{4,0},{5,1},{6,22},{7,23},{8,12},{9,13},... | collective-permute-start | bytes 786440 | tf_op jit(solution)/shard_map/ppermute | solution.py:32
  13.9 0.0 copy-done.1
  13.9 0.1 copy.10
  14.0 0.5 copy.8
  14.5 1.0 %reshape.167.qt_ref = bf16[2,128,1024]{2,1,0:T(8,128)(2,1)} reshape(bf16[2,128,8,128]{3,2,1,0:T(8,128)(2,1)S(1)} %bitcast.31) | data formatting | bytes 1048576 | tf_op jit(solution)/shard_map/reshape | solution.py:208
  15.5 3.3 %collective-permute-done.2 = bf16[4,128,256]{2,1,0:T(8,128)(2,1)S(1)} collective-permute-done((bf16[4,128,256]{2,1,0:T(8,128)(2,1)S(1)}, bf16[4,128,256]{2,1,0:T(8,128)(2,1)S(1)}, u32[]{:S(2)}, u32[]{:S(2)}) %collective-permute-start.2) | collective-permute-done | bytes 262176 | tf_op jit(solution)/shard_map/ppermute | solution.py:32
  18.8 0.0 copy-start.2
  18.8 0.0 copy-start.4
  18.8 1.6 %collective-permute-start.4 = (bf16[8,128,256]{2,1,0:T(8,128)(2,1)S(1)}, bf16[8,128,256]{2,1,0:T(8,128)(2,1)S(1)}, u32[]{:S(2)}, u32[]{:S(2)}) collective-permute-start(bf16[8,128,256]{2,1,0:T(8,128)(2,1)S(1)} %pad_maximum_fusion.rest_0_), channel_id=1, source_target_pairs={{0,1},{1,0},{2,10},{3,11},{4,5},{5,4},{6,14},{7,15},{8,9},{9,8},{1... | collective-permute-start | bytes 1572872 | tf_op jit(solution)/shard_map/ppermute | solution.py:32
  20.4 0.1 bitcast_reduce_fusion.1
  20.6 0.5 copy-done.7
  21.1 0.2 fusion
  21.3 0.1 collective-permute-start.3
  21.3 6.8 %collective-permute-done.4.rest_0_ = bf16[8,128,256]{2,1,0:T(8,128)(2,1)S(1)} collective-permute-done((bf16[8,128,256]{2,1,0:T(8,128)(2,1)S(1)}, bf16[8,128,256]{2,1,0:T(8,128)(2,1)S(1)}, u32[]{:S(2)}, u32[]{:S(2)}) %collective-permute-start.4) | collective-permute-done | bytes 524320 | tf_op jit(solution)/shard_map/ppermute | solution.py:32
  28.1 0.0 collective-permute-start.5
  28.1 0.7 %pad_add_fusion.info_ref = s32[3,2]{1,0:T(4,128)} fusion(s32[1,2]{1,0:T(1,128)S(1)} %get-tuple-element.21, s32[1,2]{1,0:T(1,128)S(1)} %get-tuple-element.22, s32[1,2]{1,0:T(1,128)S(1)} %bitcast.45), kind=kLoop, calls=%fused_computation.7 | loop fusion | flops 12 | bytes 48 | tf_op jit(solution)/shard_map/stack | solution.py:202
  28.8 0.1 select_reduce_fusion.1
  28.9 0.8 %select_reduce_fusion.slot_ref = s32[32]{0:T(128)} fusion(s32[32]{0:T(128)S(1)} %compare_select_fusion, s32[32]{0:T(128)S(1)} %select_reduce_fusion.1), kind=kLoop, calls=%fused_computation.4 | loop fusion | flops 3040 | bytes 384 | tf_op jit(solution)/shard_map/reduce_sum | solution.py:191
  29.7 5.6 %shard_map.55 = (f32[2,1,1024]{2,1,0:T(1,128)}, f32[2,1,1024]{2,1,0:T(1,128)}, f32[2,128,1024]{2,1,0:T(8,128)}) custom-call(s32[3,2]{1,0:T(4,128)} %pad_add_fusion.info_ref, s32[32]{0:T(128)} %select_reduce_fusion.slot_ref, bf16[2,128,1024]{2,1,0:T(8,128)(2,1)} %reshape.167.qt_ref, bf16[8,128,256]{2,1,0:T(8,128)(2,1)} %copy-done.2, s32[2,1,128]{2,1,0:T(1,128)} %bitcast.42), custom_call_target="tpu_custom_call" | custom-call | flops 570425344 | bytes 1572864 | tf_op jit(solution)/shard_map/pallas_call | solution.py:242
  35.2 5.4 %shard_map.56 = (f32[2,1,1024]{2,1,0:T(1,128)}, f32[2,1,1024]{2,1,0:T(1,128)}, f32[2,128,1024]{2,1,0:T(8,128)}) custom-call(s32[3,2]{1,0:T(4,128)} %pad_add_fusion.info_ref, s32[32]{0:T(128)} %select_reduce_fusion.slot_ref, bf16[2,128,1024]{2,1,0:T(8,128)(2,1)} %reshape.167.qt_ref, bf16[8,128,256]{2,1,0:T(8,128)(2,1)} %copy-done, s32[2,1,128]{2,1,0:T(1,128)} %bitcast.43, ...), custom_call_target="tpu_custom_call" | custom-call | flops 570425344 | bytes 1572864 | tf_op jit(solution)/shard_map/pallas_call | solution.py:242
  40.6 0.0 collective-permute-done.3.rest_0_
  40.7 0.0 collective-permute-done.5.rest_1_
  40.7 0.0 copy-start.6
  40.7 0.8 %copy-done.5 = bf16[8,128,256]{2,1,0:T(8,128)(2,1)} copy-done((bf16[8,128,256]{2,1,0:T(8,128)(2,1)}, bf16[8,128,256]{2,1,0:T(8,128)(2,1)S(1)}, u32[]{:S(2)}) %copy-start.5) | copy-done | bytes 524312
  41.5 0.2 copy-done.6
  41.6 10.4 %shard_map.57 = (f32[2,1,1024]{2,1,0:T(1,128)}, f32[2,1,1024]{2,1,0:T(1,128)}, f32[2,128,1024]{2,1,0:T(8,128)}, bf16[256,1024]{1,0:T(8,128)(2,1)}) custom-call(s32[3,2]{1,0:T(4,128)} %pad_add_fusion.info_ref, s32[32]{0:T(128)} %select_reduce_fusion.slot_ref, bf16[2,128,1024]{2,1,0:T(8,128)(2,1)} %reshape.167.qt_ref, bf16[8,128,256]{2,1,0:T(8,128)(2,1)} %copy-done.5, ...), custom_call_target="tpu_custom_call" | custom-call | flops 1140850688 | bytes 2097152 | tf_op jit(solution)/shard_map/pallas_call | solution.py:242
  (15 shorter events, 0.1 us)
Async XLA Ops:
  0.0 0.9 %copy-start.3 = (bf16[128,128]{1,0:T(8,128)(2,1)S(1)}, bf16[128,128]{1,0:T(8,128)(2,1)}, u32[]{:S(2)}) copy-start(bf16[128,128]{1,0:T(8,128)(2,1)} %param.6) | copy-start | bytes 98308
  0.0 13.9 %copy-start.1 = (bf16[256,1024]{1,0:T(8,128)(2,1)S(1)}, bf16[256,1024]{1,0:T(8,128)(2,1)}, u32[]{:S(2)}) copy-start(bf16[256,1024]{1,0:T(8,128)(2,1)} %param.5) | copy-start | bytes 1572868
  1.0 5.3 %collective-permute-start = (bf16[1,128,256]{2,1,0:T(8,128)(2,1)S(1)}, bf16[1,128,256]{2,1,0:T(8,128)(2,1)S(1)}, u32[]{:S(2)}, u32[]{:S(2)}) collective-permute-start(bf16[1,128,256]{2,1,0:T(8,128)(2,1)S(1)} %pad_maximum_fusion.3), channel_id=1, source_target_pairs={{0,16},{1,17},{2,3},{3,2},{4,20},{5,21},{6,7},{7,6},{8,24},{9,25},... | collective-permute-start | bytes 196616 | tf_op jit(solution)/shard_map/ppermute | solution.py:32
  6.3 6.1 %collective-permute-start.1 = (bf16[2,128,256]{2,1,0:T(8,128)(2,1)S(1)}, bf16[2,128,256]{2,1,0:T(8,128)(2,1)S(1)}, u32[]{:S(2)}, u32[]{:S(2)}) collective-permute-start(bf16[2,128,256]{2,1,0:T(8,128)(2,1)S(1)} %pad_maximum_fusion.2), channel_id=1, source_target_pairs={{0,8},{1,9},{2,6},{3,7},{4,12},{5,13},{6,2},{7,3},{8,0},{9,1},{10,... | collective-permute-start | bytes 393224 | tf_op jit(solution)/shard_map/ppermute | solution.py:32
  12.3 6.4 %collective-permute-start.2 = (bf16[4,128,256]{2,1,0:T(8,128)(2,1)S(1)}, bf16[4,128,256]{2,1,0:T(8,128)(2,1)S(1)}, u32[]{:S(2)}, u32[]{:S(2)}) collective-permute-start(bf16[4,128,256]{2,1,0:T(8,128)(2,1)S(1)} %pad_maximum_fusion.1), channel_id=1, source_target_pairs={{0,4},{1,5},{2,18},{3,19},{4,0},{5,1},{6,22},{7,23},{8,12},{9,13},... | collective-permute-start | bytes 786440 | tf_op jit(solution)/shard_map/ppermute | solution.py:32
  18.8 10.8 %copy-start.2 = (bf16[8,128,256]{2,1,0:T(8,128)(2,1)}, bf16[8,128,256]{2,1,0:T(8,128)(2,1)S(1)}, u32[]{:S(2)}) copy-start(bf16[8,128,256]{2,1,0:T(8,128)(2,1)S(1)} %pad_maximum_fusion.rest_0_) | copy-start | bytes 1572868
  18.8 1.6 %copy-start.4 = (s32[256]{0:T(256)S(1)}, s32[256]{0:T(256)}, u32[]{:S(2)}) copy-start(s32[256]{0:T(256)} %param.9) | copy-start | bytes 3076
  18.8 9.2 %collective-permute-start.4 = (bf16[8,128,256]{2,1,0:T(8,128)(2,1)S(1)}, bf16[8,128,256]{2,1,0:T(8,128)(2,1)S(1)}, u32[]{:S(2)}, u32[]{:S(2)}) collective-permute-start(bf16[8,128,256]{2,1,0:T(8,128)(2,1)S(1)} %pad_maximum_fusion.rest_0_), channel_id=1, source_target_pairs={{0,1},{1,0},{2,10},{3,11},{4,5},{5,4},{6,14},{7,15},{8,9},{9,8},{1... | collective-permute-start | bytes 1572872 | tf_op jit(solution)/shard_map/ppermute | solution.py:32
  20.4 0.7 %copy-start.7 = (s32[32]{0:T(128)S(1)}, s32[32]{0:T(128)}, u32[]{:S(2)}) copy-start(s32[32]{0:T(128)} %param.8) | copy-start | bytes 388
  21.3 19.4 %collective-permute-start.3 = (bf16[8,128,256]{2,1,0:T(8,128)(2,1)S(1)}, bf16[8,128,256]{2,1,0:T(8,128)(2,1)S(1)}, u32[]{:S(2)}, u32[]{:S(2)}) collective-permute-start(bf16[8,128,256]{2,1,0:T(8,128)(2,1)S(1)} %pad_maximum_fusion.rest_0_), channel_id=1, source_target_pairs={{0,2},{1,3},{2,0},{3,1},{4,6},{5,7},{6,4},{7,5},{8,10},{9,11},{10,... | collective-permute-start | bytes 1572872 | tf_op jit(solution)/shard_map/ppermute | solution.py:39
  28.1 7.1 %copy-start = (bf16[8,128,256]{2,1,0:T(8,128)(2,1)}, bf16[8,128,256]{2,1,0:T(8,128)(2,1)S(1)}, u32[]{:S(2)}) copy-start(bf16[8,128,256]{2,1,0:T(8,128)(2,1)S(1)} %collective-permute-done.4.rest_0_) | copy-start | bytes 1572868
  28.1 12.6 %collective-permute-start.5 = (bf16[8,128,256]{2,1,0:T(8,128)(2,1)S(1)}, bf16[8,128,256]{2,1,0:T(8,128)(2,1)S(1)}, u32[]{:S(2)}, u32[]{:S(2)}) collective-permute-start(bf16[8,128,256]{2,1,0:T(8,128)(2,1)S(1)} %collective-permute-done.4.rest_0_), channel_id=1, source_target_pairs={{0,2},{1,3},{2,0},{3,1},{4,6},{5,7},{6,4},{7,5},{8,10},{9,11},{10,... | collective-permute-start | bytes 1572872 | tf_op jit(solution)/shard_map/ppermute | solution.py:39
  40.6 0.8 %copy-start.5 = (bf16[8,128,256]{2,1,0:T(8,128)(2,1)}, bf16[8,128,256]{2,1,0:T(8,128)(2,1)S(1)}, u32[]{:S(2)}) copy-start(bf16[8,128,256]{2,1,0:T(8,128)(2,1)S(1)} %collective-permute-done.3.rest_0_) | copy-start | bytes 1572868
  40.7 1.0 %copy-start.6 = (bf16[8,128,256]{2,1,0:T(8,128)(2,1)}, bf16[8,128,256]{2,1,0:T(8,128)(2,1)S(1)}, u32[]{:S(2)}) copy-start(bf16[8,128,256]{2,1,0:T(8,128)(2,1)S(1)} %collective-permute-done.5.rest_1_) | copy-start | bytes 1572868
